TPU v7x, 128 devices: a whole 4x4x4 slice. The times are simulated.
128 devices in a mesh: chan: 4 (over z_lo, core), blk: 32 (over z_hi, y, x).
Axes of the slice: x: 4, y: 4, z: 4 (z_hi: 2, z_lo: 2; z = z_hi * 2 + z_lo), core: 2. Of those that a mesh axis runs over, the one named last changes fastest.
Arguments:
- voltages: bfloat16 [256, 262144], P('blk', 'chan'), may hold values from -6 to 6
- fir_taps: float32 [8, 4096], replicated, may hold values from -2.1 to 2.1
Outputs:
- visibilities: float32 [2, 256, 256, 2048], P(None, 'blk', None, 'chan')
All inputs are finite; a program needn't handle non-finite values.
Results may differ from a plain program's by a relative error of at most 0.0036.
Values may be sent and summed in bfloat16 or wider, within the bound.
No kernel may reach another device: no remote copies, remote signals or barrier semaphores. Data moves between devices by JAX's collectives and lax.ppermute only.
A program may use at most 192 MiB of HBM per device.

v0:
```python
import math

import jax
import jax.numpy as jnp
from jax import lax
from jax.sharding import PartitionSpec as P

TAPS = 8
L = 4096
C = 2048


def shifted(value, axis, steps):
    count = lax.axis_size(axis)
    leading, last = (max(0, -steps), min(count, count - steps))
    return lax.ppermute(value, axis, [(source, source + steps) for source in range(leading, last)])


def dft_table(first_channel, channel_count, length):
    channel_ids = first_channel + jnp.arange(channel_count, dtype=jnp.int32)
    sample_ids = jnp.arange(length, dtype=jnp.int32)
    phase_index = sample_ids[:, None] * channel_ids[None, :] % length
    angles = phase_index.astype(jnp.float32) * (2.0 * math.pi / length)
    normaliser = 1.0 / math.sqrt(length)
    return jnp.concatenate([jnp.cos(angles) * normaliser, -jnp.sin(angles) * normaliser], axis=1)


def correlate_pair(left_block, right_block, inverse_count):
    gram_terms = jnp.einsum(
        "itpc,jtqc->ipjqc", left_block, right_block, preferred_element_type=jnp.float32
    )
    real_part = gram_terms[:, 0, :, 0] + gram_terms[:, 1, :, 1]
    imag_part = gram_terms[:, 1, :, 0] - gram_terms[:, 0, :, 1]
    return jnp.stack([real_part, imag_part]) * inverse_count


def on_device(voltages, fir_taps):
    feed_count = voltages.shape[0]
    frame_count = voltages.shape[1] // L
    own_frames = voltages.reshape(feed_count, frame_count, L)
    last_frames = own_frames[:, frame_count - (TAPS - 1) :, :]
    earlier = shifted(last_frames, "chan", 1)
    extended = jnp.concatenate([earlier, own_frames], axis=1)
    filtered = jnp.zeros((feed_count, frame_count, L), jnp.float32)
    for tap_index in range(TAPS):
        filtered = filtered + fir_taps[tap_index][None, None, :] * extended[
            :, tap_index : tap_index + frame_count, :
        ].astype(jnp.float32)
    frame_rows = filtered.reshape(feed_count * frame_count, L)
    block_width = min(C, 512)
    pieces = []
    for first_channel in range(0, C, block_width):
        cos_sin_table = dft_table(first_channel, block_width, L)
        product = jnp.dot(
            frame_rows,
            cos_sin_table,
            precision=lax.Precision.HIGHEST,
            preferred_element_type=jnp.float32,
        )
        pieces.append(product.reshape(feed_count * frame_count, 2, block_width))
    spectra = (
        jnp.concatenate(pieces, axis=2).astype(jnp.bfloat16).reshape(feed_count, frame_count, 2, C)
    )
    own_block = lax.all_to_all(spectra, "chan", split_axis=3, concat_axis=1, tiled=True)
    inverse_count = 1.0 / own_block.shape[1]
    return correlate_pair(
        own_block, lax.all_gather(own_block, "blk", axis=0, tiled=True), inverse_count
    )


def solution(mesh):
    placed = (P("blk", "chan"), P())
    return jax.shard_map(
        on_device,
        mesh=mesh,
        in_specs=placed,
        out_specs=P(None, "blk", None, "chan"),
        check_vma=False,
    )
```

profile of v0, /device:TPU:0, one launch (start us, length us, event | category | flops | bytes accessed | tf_op | source)
XLA Modules:
  0.0 1170.2 jit_solution(16669685366088658176)
XLA Ops:
  10.6 33.0 %negate_multiply_fusion.3 = (f32[4096,512]{0,1:T(8,128)S(1)}, f32[4096,512]{0,1:T(8,128)S(1)}) fusion(), kind=kLoop, calls=%fused_computation.44 | loop fusion | flops 35651584 | bytes 16777216 | tf_op jit(solution)/shard_map/mul | solution.py:25
  43.7 33.8 %cosine_multiply_fusion = (f32[4096,512]{0,1:T(8,128)S(1)}, f32[4096,512]{0,1:T(8,128)S(1)}) fusion(s32[512]{0:T(512)S(1)} %iota_add_fusion), kind=kLoop, calls=%fused_computation.33 | loop fusion | flops 35651584 | bytes 16779264 | tf_op jit(solution)/shard_map/mul | solution.py:25
  77.5 37.2 %cosine_multiply_fusion.1 = (f32[4096,512]{0,1:T(8,128)}, f32[4096,512]{0,1:T(8,128)}) fusion(s32[512]{0:T(512)S(1)} %iota_add_fusion.1), kind=kLoop, calls=%fused_computation.37 | loop fusion | flops 35651584 | bytes 16779264 | tf_op jit(solution)/shard_map/mul | solution.py:25
  114.7 37.2 %cosine_multiply_fusion.2 = (f32[4096,512]{0,1:T(8,128)}, f32[4096,512]{0,1:T(8,128)}) fusion(s32[512]{0:T(512)S(1)} %iota_add_fusion.2), kind=kLoop, calls=%fused_computation.41 | loop fusion | flops 35651584 | bytes 16779264 | tf_op jit(solution)/shard_map/mul | solution.py:25
  151.9 6.2 pad_maximum_fusion.3
  158.2 13.7 %pad_maximum_fusion.2 = f32[4096,1024]{0,1:T(8,128)} fusion(f32[4096,512]{0,1:T(8,128)} %get-tuple-element.16, f32[4096,512]{0,1:T(8,128)} %get-tuple-element.15), kind=kLoop, calls=%fused_computation.4 | loop fusion | flops 4194304 | bytes 33554432 | tf_op jit(solution)/shard_map/concatenate | solution.py:25
  174.6 6.4 pad_maximum_fusion.1
  181.0 6.2 pad_maximum_fusion
  187.3 5.8 multiply_add_fusion
  193.2 22.5 %fusion.49 = bf16[8,16,2,512]{3,1,2,0:T(8,128)(2,1)} fusion(f32[2,512,4096,1]{2,1,0,3:T(8,128)} %bitcast.85, f32[8,16,4096]{2,1,0:T(8,128)S(1)} %multiply_add_fusion), kind=kOutput, calls=%fused_computation.82 | convolution fusion | flops 6442582016 | bytes 19136512 | tf_op jit(solution)/shard_map/dot_general | solution.py:54
  215.8 20.0 %fusion.46 = bf16[8,16,2,512]{3,1,2,0:T(8,128)(2,1)} fusion(f32[2,512,4096,1]{2,1,0,3:T(8,128)S(1)} %bitcast.88, f32[8,16,4096]{2,1,0:T(8,128)} %copy-done.2), kind=kOutput, calls=%fused_computation.81 | convolution fusion | flops 6442582016 | bytes 19136512 | tf_op jit(solution)/shard_map/dot_general | solution.py:54
  235.7 20.8 %fusion.43 = bf16[8,16,2,512]{3,1,2,0:T(8,128)(2,1)S(1)} fusion(f32[2,512,4096,1]{2,1,0,3:T(8,128)} %bitcast.89, f32[8,16,4096]{2,1,0:T(8,128)S(1)} %copy-done.3), kind=kOutput, calls=%fused_computation.80 | convolution fusion | flops 6442582016 | bytes 19136512 | tf_op jit(solution)/shard_map/dot_general | solution.py:54
  256.6 17.6 %fusion.40 = bf16[8,16,2,512]{3,1,2,0:T(8,128)(2,1)S(1)} fusion(f32[2,512,4096,1]{2,1,0,3:T(8,128)S(1)} %bitcast.92, f32[8,16,4096]{2,1,0:T(8,128)S(1)} %copy-done.3), kind=kOutput, calls=%fused_computation.79 | convolution fusion | flops 6442582016 | bytes 19136512 | tf_op jit(solution)/shard_map/dot_general | solution.py:54
  274.4 14.3 %copy.31 = bf16[8,16,2,2048]{1,2,0,3:T(2,128)(2,1)} copy(bf16[8,16,2,2048]{3,1,2,0:T(8,128)(2,1)S(1)} %pad_maximum_fusion.5) | data formatting | bytes 2097152 | tf_op jit(solution)/shard_map/concatenate | solution.py:62
  288.7 10.2 reshape.89
  298.9 17.5 %all_to_all.18 = bf16[4,2,65536]{2,1,0:T(2,128)(2,1)S(1)} all-to-all(bf16[4,2,65536]{2,1,0:T(2,128)(2,1)S(1)} %reshape.89), channel_id=1, replica_groups=mesh['chan'=4,'blk'=32] {'chan'}, dimensions={0} | all-to-all | bytes 2097152 | tf_op jit(solution)/shard_map/all_to_all | solution.py:64
  316.4 7.1 reshape.90
  323.5 19.1 %copy.42 = bf16[8,16,2,4,512]{4,3,1,2,0:T(4,128)(2,1)S(1)} copy(bf16[8,16,2,4,512]{1,2,0,4,3:T(2,128)(2,1)} %bitcast.84) | data formatting | bytes 2097152 | tf_op jit(solution)/shard_map/all_to_all | solution.py:64
  347.8 761.5 %all-gather.2.cloned.1.call-done = bf16[256,64,2,512]{1,0,2,3:T(8,128)(2,1)} async-done(((bf16[8,64,2,512]{1,0,2,3:T(8,128)(2,1)}), bf16[256,64,2,512]{1,0,2,3:T(8,128)(2,1)}) %all-gather.2.cloned.1.call-update) | async-done | bytes 33554448 | tf_op jit(solution)/shard_map/all_gather | solution.py:67
  1109.2 32.0 %fusion.2 = f32[8,2,256,2,512]{2,0,1,3,4:T(8,128)} fusion(bf16[8,64,2,512,1]{1,0,2,4,3:T(8,128)(2,1)S(1)} %copy.41, bf16[256,64,2,512]{1,0,2,3:T(8,128)(2,1)} %all-gather.2.cloned.1.call-done), kind=kOutput, calls=%fused_computation.18 | convolution fusion | flops 536870912 | bytes 51380224 | tf_op jit(solution)/shard_map/itpc,jtqc->ipjqc/dot_general | solution.py:29
  1141.2 4.0 fusion.29
  1145.2 4.0 fusion.31
  1149.2 3.8 maximum_multiply_fusion
  1153.0 9.9 copy.38
  (46 shorter events, 12.2 us)
Async XLA Ops:
  6.5 1102.7 %all-gather.2.cloned.1.call-start = ((), (), s32[]{:S(2)}) async-start(), calls=%async_computation.1 | async-start | bytes 69206016 | tf_op jit(solution)/shard_map/all_gather | solution.py:67
  8.5 178.8 %collective-permute-start = (bf16[8,7,4096]{2,1,0:T(8,128)(2,1)S(1)}, bf16[8,7,4096]{2,1,0:T(8,128)(2,1)}, u32[]{:S(2)}, u32[]{:S(2)}) collective-permute-start(bf16[8,7,4096]{2,1,0:T(8,128)(2,1)S(1)} %slice.80), channel_id=1, source_target_pairs={{0,32},{32,64},{64,96},{1,33},{33,65},{65,97},{2,34},{34,66},{66,9... | collective-permute-start | bytes 1376264 | tf_op jit(solution)/shard_map/ppermute | solution.py:16
  10.6 33.0 %copy-start.6 = (f32[8,4096]{1,0:T(8,128)S(1)}, f32[8,4096]{1,0:T(8,128)}, u32[]{:S(2)}) copy-start(f32[8,4096]{1,0:T(8,128)} %param.3) | copy-start | bytes 393220
  158.2 13.7 %copy-start = (f32[4096,512]{0,1:T(8,128)S(1)}, f32[4096,512]{0,1:T(8,128)}, u32[]{:S(2)}) copy-start(f32[4096,512]{0,1:T(8,128)} %get-tuple-element.13) | copy-start | bytes 25165828
  158.2 16.5 %copy-start.1 = (f32[4096,512]{0,1:T(8,128)S(1)}, f32[4096,512]{0,1:T(8,128)}, u32[]{:S(2)}) copy-start(f32[4096,512]{0,1:T(8,128)} %get-tuple-element.14) | copy-start | bytes 25165828
  187.3 28.4 %slice-start = ((s8[16777216]{0:T(1024)(128)(4,1)}), s8[4194304]{0:T(1024)(128)(4,1)S(1)}, s32[]{:S(2)}) async-start(s8[16777216]{0:T(1024)(128)(4,1)} %bitcast.86), calls=%async_computation.2 | async-start | bytes 8388608
  193.1 22.5 %copy-start.2 = (f32[8,16,4096]{2,1,0:T(8,128)}, f32[8,16,4096]{2,1,0:T(8,128)S(1)}, u32[]{:S(2)}) copy-start(f32[8,16,4096]{2,1,0:T(8,128)S(1)} %multiply_add_fusion) | copy-start | bytes 6291460
  193.1 22.5 %slice-start.1 = ((s8[16777216]{0:T(1024)(128)(4,1)}), s8[4194304]{0:T(1024)(128)(4,1)S(1)}, s32[]{:S(2)}) async-start(s8[16777216]{0:T(1024)(128)(4,1)} %bitcast.86), calls=%async_computation.3 | async-start | bytes 8388608
  193.2 22.5 %slice-start.2 = ((s8[16777216]{0:T(1024)(128)(4,1)}), s8[4194304]{0:T(1024)(128)(4,1)S(1)}, s32[]{:S(2)}) async-start(s8[16777216]{0:T(1024)(128)(4,1)} %bitcast.86), calls=%async_computation.4 | async-start | bytes 8388608
  193.2 22.5 %slice-start.3 = ((s8[16777216]{0:T(1024)(128)(4,1)}), s8[4194304]{0:T(1024)(128)(4,1)S(1)}, s32[]{:S(2)}) async-start(s8[16777216]{0:T(1024)(128)(4,1)} %bitcast.86), calls=%async_computation.5 | async-start | bytes 8388608
  215.7 20.0 %copy-start.3 = (f32[8,16,4096]{2,1,0:T(8,128)S(1)}, f32[8,16,4096]{2,1,0:T(8,128)}, u32[]{:S(2)}) copy-start(f32[8,16,4096]{2,1,0:T(8,128)} %copy-done.2) | copy-start | bytes 6291460
  215.7 40.8 %slice-start.4 = ((s8[16777216]{0:T(1024)(128)(4,1)}), s8[4194304]{0:T(1024)(128)(4,1)S(1)}, s32[]{:S(2)}) async-start(s8[16777216]{0:T(1024)(128)(4,1)} %bitcast.90), calls=%async_computation.6 | async-start | bytes 8388608
  215.7 40.8 %slice-start.5 = ((s8[16777216]{0:T(1024)(128)(4,1)}), s8[4194304]{0:T(1024)(128)(4,1)S(1)}, s32[]{:S(2)}) async-start(s8[16777216]{0:T(1024)(128)(4,1)} %bitcast.90), calls=%async_computation.7 | async-start | bytes 8388608
  235.7 20.8 %slice-start.6 = ((s8[16777216]{0:T(1024)(128)(4,1)}), s8[4194304]{0:T(1024)(128)(4,1)S(1)}, s32[]{:S(2)}) async-start(s8[16777216]{0:T(1024)(128)(4,1)} %bitcast.90), calls=%async_computation.8 | async-start | bytes 8388608
  235.7 20.8 %slice-start.7 = ((s8[16777216]{0:T(1024)(128)(4,1)}), s8[4194304]{0:T(1024)(128)(4,1)S(1)}, s32[]{:S(2)}) async-start(s8[16777216]{0:T(1024)(128)(4,1)} %bitcast.90), calls=%async_computation.9 | async-start | bytes 8388608
  256.6 17.6 %copy-start.4 = (bf16[8,16,2,512]{3,1,2,0:T(8,128)(2,1)S(1)}, bf16[8,16,2,512]{3,1,2,0:T(8,128)(2,1)}, u32[]{:S(2)}) copy-start(bf16[8,16,2,512]{3,1,2,0:T(8,128)(2,1)} %fusion.49) | copy-start | bytes 786436
  256.6 17.6 %copy-start.5 = (bf16[8,16,2,512]{3,1,2,0:T(8,128)(2,1)S(1)}, bf16[8,16,2,512]{3,1,2,0:T(8,128)(2,1)}, u32[]{:S(2)}) copy-start(bf16[8,16,2,512]{3,1,2,0:T(8,128)(2,1)} %fusion.46) | copy-start | bytes 786436
Sparse Core Ops, SparseCore 0:
  345.8 763.3 all-gather.1
where the time goes:
time: 1180 us; the launch traced here: 1170 us
  waiting for transfers between devices  761 us (64%)
  other arithmetic  192 us (16%)
  matrix products  113 us (10%)
  local copies, waits for them, and re-layouts  70.6 us (6%)
  blocking collectives  17.5 us (1%)
  between operations  14.1 us (1%)
    all_gather x1, waiting for transfers between devices, on_device(): lax.all_gather(own_block, 'blk', axis=0, tiled=True)  761 us
    mul x3, other arithmetic, dft_table(): jnp.cos(angles) * normaliser  108 us
    dot_general x4, matrix products, on_device(): jnp.dot(frame_rows, cos_sin_table, precision=lax.Precision.HIGHEST, prefe...  80.8 us
    mul x1, other arithmetic, dft_table(): -jnp.sin(angles) * normaliser  33 us
    concatenate x4, other arithmetic, dft_table(): jnp.concatenate([jnp.cos(angles) * normaliser, -jnp.sin(angles) * normali...  32.6 us
    dot_general x1, matrix products, correlate_pair(): jnp.einsum('itpc,jtqc->ipjqc', left_block, right_block, preferred_element...  32 us
    all_to_all x4, local copies, waits for them, and re-layouts, on_device(): lax.all_to_all(spectra, 'chan', split_axis=3, concat_axis=1, tiled=True)  24.2 us
  transfers between devices with their start and end apart: 2, of which 1 were waited for; matrix products, arithmetic and copies ran while one was open for 15% of the time, Pallas kernels for 0%

commit v1 on v0

--- a/solution.py
+++ b/solution.py
@@ -3,6 +3,7 @@
 import jax
 import jax.numpy as jnp
 from jax import lax
+from jax.experimental.layout import Layout, with_layout_constraint
 from jax.sharding import PartitionSpec as P
 
 TAPS = 8
@@ -25,13 +26,15 @@
     return jnp.concatenate([jnp.cos(angles) * normaliser, -jnp.sin(angles) * normaliser], axis=1)
 
 
-def correlate_pair(left_block, right_block, inverse_count):
-    gram_terms = jnp.einsum(
-        "itpc,jtqc->ipjqc", left_block, right_block, preferred_element_type=jnp.float32
+def correlate(own_block, every_block, inverse_count):
+    real_part, imag_part = own_block[:, 0], own_block[:, 1]
+    paired = jnp.stack(
+        [jnp.stack([real_part, imag_part], axis=1), jnp.stack([imag_part, -real_part], axis=1)]
     )
-    real_part = gram_terms[:, 0, :, 0] + gram_terms[:, 1, :, 1]
-    imag_part = gram_terms[:, 1, :, 0] - gram_terms[:, 0, :, 1]
-    return jnp.stack([real_part, imag_part]) * inverse_count
+    products = jnp.einsum(
+        "riptc,jptc->rijc", paired, every_block, preferred_element_type=jnp.float32
+    )
+    return products * inverse_count
 
 
 def on_device(voltages, fir_taps):
@@ -63,9 +66,14 @@
     )
     own_block = lax.all_to_all(spectra, "chan", split_axis=3, concat_axis=1, tiled=True)
     inverse_count = 1.0 / own_block.shape[1]
-    return correlate_pair(
-        own_block, lax.all_gather(own_block, "blk", axis=0, tiled=True), inverse_count
+    own_block = own_block.transpose(0, 2, 1, 3)
+    row_major = Layout(major_to_minor=tuple(range(own_block.ndim + 1)))
+    local = with_layout_constraint(own_block[None], row_major)
+    gathered = with_layout_constraint(
+        lax.all_gather(local, "blk", axis=0, tiled=True), row_major
     )
+    every_block = gathered.reshape((-1,) + own_block.shape[1:])
+    return correlate(own_block, every_block, inverse_count)
 
 
 def solution(mesh):

time: 1180 us -> 700 us (0.59)
  waiting for transfers between devices: 761 us -> 254 us
  local copies, waits for them, and re-layouts: 70.6 us -> 123 us
  matrix products: 113 us -> 97.9 us
    all_gather x1, waiting for transfers between devices: 761 us -> 254 us  [on_device(): lax.all_gather(local, 'blk', axis=0, tiled=True)]
    reshape x0 -> x1, local copies, waits for them, and re-layouts: none -> 50.8 us  [on_device(): every_block = gathered.reshape((-1,) + own_block.shape[1:])]
    dot_general x1, matrix products: 32 us -> 17.2 us  [correlate(): jnp.einsum('riptc,jptc->rijc', paired, every_block, preferred_element_typ...]
    all_to_all x4 -> x1, local copies, waits for them, and re-layouts: 24.2 us -> 19.3 us  [on_device(): lax.all_to_all(spectra, 'chan', split_axis=3, concat_axis=1, tiled=True)]
  transfers between devices with their start and end apart: 2 -> 2, of which waited for: 1 -> 1; matrix products, arithmetic and copies ran while one was open for 15% -> 27% of each run, Pallas kernels for 0% -> 0%
where the time goes in v1:
time: 700 us; the launch traced here: 691 us
  waiting for transfers between devices  254 us (36%)
  other arithmetic  183 us (26%)
  local copies, waits for them, and re-layouts  123 us (18%)
  matrix products  97.9 us (14%)
  blocking collectives  17.5 us (2%)
  between operations  13.9 us (2%)
    all_gather x1, waiting for transfers between devices, on_device(): lax.all_gather(local, 'blk', axis=0, tiled=True)  254 us
    mul x3, other arithmetic, dft_table(): jnp.cos(angles) * normaliser  108 us
    dot_general x4, matrix products, on_device(): jnp.dot(frame_rows, cos_sin_table, precision=lax.Precision.HIGHEST, prefe...  80.8 us
    reshape x1, local copies, waits for them, and re-layouts, on_device(): every_block = gathered.reshape((-1,) + own_block.shape[1:])  50.8 us
    concatenate x4, other arithmetic, dft_table(): jnp.concatenate([jnp.cos(angles) * normaliser, -jnp.sin(angles) * normali...  33.3 us
    mul x1, other arithmetic, dft_table(): -jnp.sin(angles) * normaliser  33 us
    unnamed x32, local copies, waits for them, and re-layouts  20.1 us
    all_to_all x1, local copies, waits for them, and re-layouts, on_device(): lax.all_to_all(spectra, 'chan', split_axis=3, concat_axis=1, tiled=True)  19.3 us
  transfers between devices with their start and end apart: 2, of which 1 were waited for; matrix products, arithmetic and copies ran while one was open for 27% of the time, Pallas kernels for 0%

profile of v1, /device:TPU:0, one launch (start us, length us, event | category | flops | bytes accessed | tf_op | source)
XLA Modules:
  0.0 691.1 jit_solution(8309814555249872896)
XLA Ops:
  10.6 33.0 %negate_multiply_fusion.3 = (f32[4096,512]{0,1:T(8,128)S(1)}, f32[4096,512]{0,1:T(8,128)S(1)}) fusion(), kind=kLoop, calls=%fused_computation.42 | loop fusion | flops 35651584 | bytes 16777216 | tf_op jit(solution)/shard_map/mul | solution.py:26
  43.7 33.5 %cosine_multiply_fusion = (f32[4096,512]{0,1:T(8,128)S(1)}, f32[4096,512]{0,1:T(8,128)S(1)}) fusion(s32[512]{0:T(512)S(1)} %iota_add_fusion), kind=kLoop, calls=%fused_computation.31 | loop fusion | flops 35651584 | bytes 16779264 | tf_op jit(solution)/shard_map/mul | solution.py:26
  77.3 37.2 %cosine_multiply_fusion.1 = (f32[4096,512]{0,1:T(8,128)}, f32[4096,512]{0,1:T(8,128)}) fusion(s32[512]{0:T(512)S(1)} %iota_add_fusion.1), kind=kLoop, calls=%fused_computation.35 | loop fusion | flops 35651584 | bytes 16779264 | tf_op jit(solution)/shard_map/mul | solution.py:26
  114.5 37.2 %cosine_multiply_fusion.2 = (f32[4096,512]{0,1:T(8,128)}, f32[4096,512]{0,1:T(8,128)}) fusion(s32[512]{0:T(512)S(1)} %iota_add_fusion.2), kind=kLoop, calls=%fused_computation.39 | loop fusion | flops 35651584 | bytes 16779264 | tf_op jit(solution)/shard_map/mul | solution.py:26
  151.7 6.4 pad_maximum_fusion.3
  158.1 13.7 %pad_maximum_fusion.2 = f32[4096,1024]{0,1:T(8,128)} fusion(f32[4096,512]{0,1:T(8,128)} %get-tuple-element.18, f32[4096,512]{0,1:T(8,128)} %get-tuple-element.17), kind=kLoop, calls=%fused_computation.2 | loop fusion | flops 4194304 | bytes 33554432 | tf_op jit(solution)/shard_map/concatenate | solution.py:26
  171.8 2.7 copy-done.1
  174.5 6.8 pad_maximum_fusion.1
  181.3 6.4 pad_maximum_fusion
  187.7 5.6 multiply_add_fusion
  193.4 22.2 %fusion.42 = bf16[8,16,2,512]{3,1,2,0:T(8,128)(2,1)} fusion(f32[2,512,4096,1]{2,1,0,3:T(8,128)} %bitcast.79, f32[8,16,4096]{2,1,0:T(8,128)S(1)} %multiply_add_fusion), kind=kOutput, calls=%fused_computation.75 | convolution fusion | flops 6442582016 | bytes 19136512 | tf_op jit(solution)/shard_map/dot_general | solution.py:57
  215.8 20.2 %fusion.39 = bf16[8,16,2,512]{3,1,2,0:T(8,128)(2,1)} fusion(f32[2,512,4096,1]{2,1,0,3:T(8,128)S(1)} %bitcast.82, f32[8,16,4096]{2,1,0:T(8,128)} %copy-done.2), kind=kOutput, calls=%fused_computation.74 | convolution fusion | flops 6442582016 | bytes 19136512 | tf_op jit(solution)/shard_map/dot_general | solution.py:57
  236.0 20.8 %fusion.36 = bf16[8,16,2,512]{3,1,2,0:T(8,128)(2,1)S(1)} fusion(f32[2,512,4096,1]{2,1,0,3:T(8,128)} %bitcast.83, f32[8,16,4096]{2,1,0:T(8,128)S(1)} %copy-done.3), kind=kOutput, calls=%fused_computation.73 | convolution fusion | flops 6442582016 | bytes 19136512 | tf_op jit(solution)/shard_map/dot_general | solution.py:57
  256.8 17.6 %fusion.33 = bf16[8,16,2,512]{3,1,2,0:T(8,128)(2,1)S(1)} fusion(f32[2,512,4096,1]{2,1,0,3:T(8,128)S(1)} %bitcast.86, f32[8,16,4096]{2,1,0:T(8,128)S(1)} %copy-done.3), kind=kOutput, calls=%fused_computation.72 | convolution fusion | flops 6442582016 | bytes 19136512 | tf_op jit(solution)/shard_map/dot_general | solution.py:57
  274.6 14.3 %copy.13 = bf16[8,16,2,2048]{1,2,0,3:T(2,128)(2,1)} copy(bf16[8,16,2,2048]{3,1,2,0:T(8,128)(2,1)S(1)} %pad_maximum_fusion.6) | data formatting | bytes 2097152 | tf_op jit(solution)/shard_map/concatenate | solution.py:65
  288.9 10.2 %reshape.57 = bf16[4,2,65536]{2,1,0:T(2,128)(2,1)S(1)} reshape(bf16[2048,8,2,16]{3,2,1,0:T(2,128)(2,1)} %bitcast.76) | data formatting | bytes 2097152
  299.1 17.5 %all_to_all.18 = bf16[4,2,65536]{2,1,0:T(2,128)(2,1)S(1)} all-to-all(bf16[4,2,65536]{2,1,0:T(2,128)(2,1)S(1)} %reshape.57), channel_id=1, replica_groups=mesh['chan'=4,'blk'=32] {'chan'}, dimensions={0} | all-to-all | bytes 2097152 | tf_op jit(solution)/shard_map/all_to_all | solution.py:67
  316.6 7.1 %reshape.58 = bf16[2048,8,2,16]{3,2,1,0:T(2,128)(2,1)} reshape(bf16[4,2,65536]{2,1,0:T(2,128)(2,1)S(1)} %all_to_all.18) | data formatting | bytes 2097152
  323.7 19.3 %copy.14 = bf16[8,16,2,4,512]{4,1,3,2,0:T(8,128)(2,1)} copy(bf16[8,16,2,4,512]{1,2,0,4,3:T(2,128)(2,1)} %bitcast.77) | data formatting | bytes 2097152 | tf_op jit(solution)/shard_map/all_to_all | solution.py:67
  345.8 6.6 copy.16
  352.4 253.7 %all-gather.2.cloned.1.call-done = bf16[32,8,2,64,512]{4,3,2,1,0:T(8,128)(2,1)} async-done(((bf16[1,8,2,64,512]{4,3,2,1,0:T(8,128)(2,1)}), bf16[32,8,2,64,512]{4,3,2,1,0:T(8,128)(2,1)}) %all-gather.2.cloned.1.call-update) | async-done | bytes 33554448 | tf_op jit(solution)/shard_map/all_gather | solution.py:73
  606.2 50.8 %copy.19 = bf16[256,2,64,512,1]{0,2,1,4,3:T(8,128)(2,1)} copy(bf16[256,2,64,512,1]{3,2,1,0,4:T(8,128)(2,1)} %bitcast.78) | data formatting | bytes 67108864 | tf_op jit(solution)/shard_map/reshape | solution.py:75
  657.0 17.2 %fusion.12 = f32[2,8,256,512]{2,1,0,3:T(8,128)} fusion(bf16[256,2,64,512,1]{0,2,1,4,3:T(8,128)(2,1)} %copy.19, bf16[2,8,2,64,512]{3,1,2,0,4:T(8,128)(2,1)} %copy.16), kind=kOutput, calls=%fused_computation.29 | convolution fusion | flops 538968064 | bytes 44040192 | tf_op jit(solution)/shard_map/riptc,jptc->rijc/dot_general | solution.py:34
  674.1 9.9 %copy.17 = f32[2,8,256,512]{3,2,1,0:T(8,128)} copy(f32[2,8,256,512]{2,1,0,3:T(8,128)} %fusion.12) | data formatting | bytes 16777216 | tf_op jit(solution)/shard_map/mul | solution.py:37
  (45 shorter events, 7.2 us)
Async XLA Ops:
  6.5 599.7 %all-gather.2.cloned.1.call-start = ((), (), s32[]{:S(2)}) async-start(), calls=%async_computation.1 | async-start | bytes 34603008 | tf_op jit(solution)/shard_map/all_gather | solution.py:73
  8.5 179.3 %collective-permute-start = (bf16[8,7,4096]{2,1,0:T(8,128)(2,1)S(1)}, bf16[8,7,4096]{2,1,0:T(8,128)(2,1)}, u32[]{:S(2)}, u32[]{:S(2)}) collective-permute-start(bf16[8,7,4096]{2,1,0:T(8,128)(2,1)S(1)} %slice.73), channel_id=1, source_target_pairs={{0,32},{32,64},{64,96},{1,33},{33,65},{65,97},{2,34},{34,66},{66,9... | collective-permute-start | bytes 1376264 | tf_op jit(solution)/shard_map/ppermute | solution.py:17
  10.6 33.0 %copy-start.6 = (f32[8,4096]{1,0:T(8,128)S(1)}, f32[8,4096]{1,0:T(8,128)}, u32[]{:S(2)}) copy-start(f32[8,4096]{1,0:T(8,128)} %param.3) | copy-start | bytes 393220
  158.0 13.7 %copy-start = (f32[4096,512]{0,1:T(8,128)S(1)}, f32[4096,512]{0,1:T(8,128)}, u32[]{:S(2)}) copy-start(f32[4096,512]{0,1:T(8,128)} %get-tuple-element.15) | copy-start | bytes 25165828
  158.0 16.5 %copy-start.1 = (f32[4096,512]{0,1:T(8,128)S(1)}, f32[4096,512]{0,1:T(8,128)}, u32[]{:S(2)}) copy-start(f32[4096,512]{0,1:T(8,128)} %get-tuple-element.16) | copy-start | bytes 25165828
  187.7 28.0 %slice-start = ((s8[16777216]{0:T(1024)(128)(4,1)}), s8[4194304]{0:T(1024)(128)(4,1)S(1)}, s32[]{:S(2)}) async-start(s8[16777216]{0:T(1024)(128)(4,1)} %bitcast.80), calls=%async_computation.2 | async-start | bytes 8388608
  193.4 22.3 %copy-start.2 = (f32[8,16,4096]{2,1,0:T(8,128)}, f32[8,16,4096]{2,1,0:T(8,128)S(1)}, u32[]{:S(2)}) copy-start(f32[8,16,4096]{2,1,0:T(8,128)S(1)} %multiply_add_fusion) | copy-start | bytes 6291460
  193.4 22.3 %slice-start.1 = ((s8[16777216]{0:T(1024)(128)(4,1)}), s8[4194304]{0:T(1024)(128)(4,1)S(1)}, s32[]{:S(2)}) async-start(s8[16777216]{0:T(1024)(128)(4,1)} %bitcast.80), calls=%async_computation.3 | async-start | bytes 8388608
  193.4 22.3 %slice-start.2 = ((s8[16777216]{0:T(1024)(128)(4,1)}), s8[4194304]{0:T(1024)(128)(4,1)S(1)}, s32[]{:S(2)}) async-start(s8[16777216]{0:T(1024)(128)(4,1)} %bitcast.80), calls=%async_computation.4 | async-start | bytes 8388608
  193.4 22.3 %slice-start.3 = ((s8[16777216]{0:T(1024)(128)(4,1)}), s8[4194304]{0:T(1024)(128)(4,1)S(1)}, s32[]{:S(2)}) async-start(s8[16777216]{0:T(1024)(128)(4,1)} %bitcast.80), calls=%async_computation.5 | async-start | bytes 8388608
  215.7 20.2 %copy-start.3 = (f32[8,16,4096]{2,1,0:T(8,128)S(1)}, f32[8,16,4096]{2,1,0:T(8,128)}, u32[]{:S(2)}) copy-start(f32[8,16,4096]{2,1,0:T(8,128)} %copy-done.2) | copy-start | bytes 6291460
  215.8 41.0 %slice-start.4 = ((s8[16777216]{0:T(1024)(128)(4,1)}), s8[4194304]{0:T(1024)(128)(4,1)S(1)}, s32[]{:S(2)}) async-start(s8[16777216]{0:T(1024)(128)(4,1)} %bitcast.84), calls=%async_computation.6 | async-start | bytes 8388608
  215.8 41.0 %slice-start.5 = ((s8[16777216]{0:T(1024)(128)(4,1)}), s8[4194304]{0:T(1024)(128)(4,1)S(1)}, s32[]{:S(2)}) async-start(s8[16777216]{0:T(1024)(128)(4,1)} %bitcast.84), calls=%async_computation.7 | async-start | bytes 8388608
  236.0 20.8 %slice-start.6 = ((s8[16777216]{0:T(1024)(128)(4,1)}), s8[4194304]{0:T(1024)(128)(4,1)S(1)}, s32[]{:S(2)}) async-start(s8[16777216]{0:T(1024)(128)(4,1)} %bitcast.84), calls=%async_computation.8 | async-start | bytes 8388608
  236.0 20.8 %slice-start.7 = ((s8[16777216]{0:T(1024)(128)(4,1)}), s8[4194304]{0:T(1024)(128)(4,1)S(1)}, s32[]{:S(2)}) async-start(s8[16777216]{0:T(1024)(128)(4,1)} %bitcast.84), calls=%async_computation.9 | async-start | bytes 8388608
  256.8 17.6 %copy-start.4 = (bf16[8,16,2,512]{3,1,2,0:T(8,128)(2,1)S(1)}, bf16[8,16,2,512]{3,1,2,0:T(8,128)(2,1)}, u32[]{:S(2)}) copy-start(bf16[8,16,2,512]{3,1,2,0:T(8,128)(2,1)} %fusion.42) | copy-start | bytes 786436
  256.8 17.6 %copy-start.5 = (bf16[8,16,2,512]{3,1,2,0:T(8,128)(2,1)S(1)}, bf16[8,16,2,512]{3,1,2,0:T(8,128)(2,1)}, u32[]{:S(2)}) copy-start(bf16[8,16,2,512]{3,1,2,0:T(8,128)(2,1)} %fusion.39) | copy-start | bytes 786436
Sparse Core Ops, SparseCore 0:
  343.1 263.0 all-gather.1

commit v2 on v1

v2 whole, which is shorter than its diff:
```python
import math

import jax
import jax.numpy as jnp
from jax import lax
from jax.experimental.layout import Layout, with_layout_constraint
from jax.sharding import PartitionSpec as P

TAPS = 8
L = 4096
C = 2048
ROOT = 64


def shifted(value, axis, steps):
    count = lax.axis_size(axis)
    leading, last = (max(0, -steps), min(count, count - steps))
    return lax.ppermute(value, axis, [(source, source + steps) for source in range(leading, last)])


def turn(rows, columns, length):
    phase_index = jnp.arange(rows, dtype=jnp.int32)[:, None] * jnp.arange(
        columns, dtype=jnp.int32
    )[None, :] % length
    angles = phase_index.astype(jnp.float32) * (2.0 * math.pi / length)
    return jnp.cos(angles), -jnp.sin(angles)


def spectra_of(frames, groups):
    rows = frames.shape[0]
    exact = lax.Precision.HIGHEST
    first_cos, first_sin = turn(ROOT, ROOT, ROOT)
    first_table = jnp.concatenate([first_cos, first_sin], axis=1) * (1.0 / math.sqrt(L))
    split = frames.reshape(rows, ROOT, ROOT)
    stage = jnp.einsum(
        "rab,ak->rkb", split, first_table, precision=exact, preferred_element_type=jnp.float32
    )
    stage_real, stage_imag = stage[:, :ROOT], stage[:, ROOT:]
    twiddle_real, twiddle_imag = turn(ROOT, ROOT, L)
    turned_real = stage_real * twiddle_real - stage_imag * twiddle_imag
    turned_imag = stage_real * twiddle_imag + stage_imag * twiddle_real
    kept = C // ROOT
    second_cos, second_sin = turn(ROOT, kept, ROOT)
    second_table = jnp.concatenate(
        [
            jnp.concatenate([second_cos, second_sin], axis=1),
            jnp.concatenate([-second_sin, second_cos], axis=1),
        ],
        axis=0,
    )
    turned = jnp.concatenate([turned_real, turned_imag], axis=2)
    product = jnp.einsum(
        "rkb,bm->rkm", turned, second_table, precision=exact, preferred_element_type=jnp.float32
    )
    per_group = kept // groups
    product = product.reshape(rows, ROOT, 2, groups, per_group)
    return product.transpose(3, 0, 2, 4, 1).reshape(groups, rows, 2, per_group * ROOT)


def correlate(own_block, every_block, inverse_count):
    real_part, imag_part = own_block[:, :, 0], own_block[:, :, 1]
    paired = jnp.stack(
        [jnp.stack([real_part, imag_part], axis=2), jnp.stack([imag_part, -real_part], axis=2)]
    )
    blocks, feeds, spans, parts, frames, width = every_block.shape
    depth = spans * parts * frames
    left = paired.reshape(2, feeds, depth, width)
    right = every_block.reshape(blocks * feeds, depth, width)
    products = jnp.einsum("rikc,jkc->rijc", left, right, preferred_element_type=jnp.float32)
    return products * inverse_count


def on_device(voltages, fir_taps):
    feed_count = voltages.shape[0]
    frame_count = voltages.shape[1] // L
    groups = lax.axis_size("chan")
    own_frames = voltages.reshape(feed_count, frame_count, L)
    last_frames = own_frames[:, frame_count - (TAPS - 1) :, :]
    earlier = shifted(last_frames, "chan", 1)
    extended = jnp.concatenate([earlier, own_frames], axis=1)
    filtered = jnp.zeros((feed_count, frame_count, L), jnp.float32)
    for tap_index in range(TAPS):
        filtered = filtered + fir_taps[tap_index][None, None, :] * extended[
            :, tap_index : tap_index + frame_count, :
        ].astype(jnp.float32)
    frame_rows = filtered.reshape(feed_count * frame_count, L)
    spectra = spectra_of(frame_rows, groups).astype(jnp.bfloat16)
    width = spectra.shape[-1]
    spectra = spectra.reshape(groups, feed_count, frame_count, 2, width).transpose(1, 0, 3, 2, 4)
    own_block = lax.all_to_all(spectra, "chan", split_axis=1, concat_axis=1, tiled=True)
    inverse_count = 1.0 / (groups * frame_count)
    row_major = Layout(major_to_minor=tuple(range(own_block.ndim + 1)))
    local = with_layout_constraint(own_block[None], row_major)
    every_block = with_layout_constraint(
        lax.all_gather(local, "blk", axis=0, tiled=True), row_major
    )
    return correlate(own_block, every_block, inverse_count)


def solution(mesh):
    placed = (P("blk", "chan"), P())
    return jax.shard_map(
        on_device,
        mesh=mesh,
        in_specs=placed,
        out_specs=P(None, "blk", None, "chan"),
        check_vma=False,
    )
```

time: 700 us -> 407 us (0.58); the launches traced: 691 us -> 405 us
  other arithmetic: 183 us -> 8.52 us
  matrix products: 97.9 us -> 26.6 us
  local copies, waits for them, and re-layouts: 123 us -> 69.2 us
  blocking collectives: 17.5 us -> 25.2 us
  waiting for transfers between devices: 254 us -> 261 us
    mul x4 -> x0, other arithmetic: 141 us -> none  [the longest x3 108 us: dft_table(): jnp.cos(angles) * normaliser]
    dot_general x5 -> x3, matrix products: 97.9 us -> 26.6 us  [the longest x1 18 us: correlate(): jnp.einsum('rikc,jkc->rijc', left, right, preferred_element_type=jnp.floa...]
    concatenate x5 -> x1, other arithmetic: 33.4 us -> 0.58 us  [spectra_of(): turned = jnp.concatenate([turned_real, turned_imag], axis=2)]
    unnamed x32 -> x6, local copies, waits for them, and re-layouts: 20.1 us -> 0.8 us
    all_to_all x1, local copies, waits for them, and re-layouts: 19.3 us -> 1.05 us  [on_device(): lax.all_to_all(spectra, 'chan', split_axis=1, concat_axis=1, tiled=True)]
    concatenate x1 -> x0, local copies, waits for them, and re-layouts: 14.3 us -> none  [on_device(): jnp.concatenate(pieces, axis=2).astype(jnp.bfloat16)]
    reshape x1, local copies, waits for them, and re-layouts: 50.8 us -> 41.9 us  [correlate(): right = every_block.reshape(blocks * feeds, depth, width)]
    all_to_all x1, blocking collectives: 17.5 us -> 25.2 us  [on_device(): lax.all_to_all(spectra, 'chan', split_axis=1, concat_axis=1, tiled=True)]
  transfers between devices with their start and end apart: 2 -> 2, of which waited for: 1 -> 2; matrix products, arithmetic and copies ran while one was open for 27% -> 1% of each run, Pallas kernels for 0% -> 0%
where the time goes in v2:
time: 407 us; the launch traced here: 405 us
  waiting for transfers between devices  261 us (64%)
  local copies, waits for them, and re-layouts  69.2 us (17%)
  matrix products  26.6 us (7%)
  blocking collectives  25.2 us (6%)
  between operations  13.6 us (3%)
  other arithmetic  8.52 us (2%)
    all_gather x1, waiting for transfers between devices, on_device(): lax.all_gather(local, 'blk', axis=0, tiled=True)  260 us
    reshape x1, local copies, waits for them, and re-layouts, correlate(): right = every_block.reshape(blocks * feeds, depth, width)  41.9 us
    all_to_all x1, blocking collectives, on_device(): lax.all_to_all(spectra, 'chan', split_axis=1, concat_axis=1, tiled=True)  25.2 us
    dot_general x1, matrix products, correlate(): jnp.einsum('rikc,jkc->rijc', left, right, preferred_element_type=jnp.floa...  18 us
    mul x1, local copies, waits for them, and re-layouts, correlate(): return products * inverse_count  9.9 us
  transfers between devices with their start and end apart: 2, of which 2 were waited for; matrix products, arithmetic and copies ran while one was open for 1% of the time, Pallas kernels for 0%

profile of v2, /device:TPU:0, one launch (start us, length us, event | category | flops | bytes accessed | tf_op | source)
XLA Modules:
  0.0 405.2 jit_solution(6650964307040657154)
XLA Ops:
  6.5 1.8 copy.37
  8.5 1.3 collective-permute-start
  10.0 0.1 fusion.41
  10.2 0.1 sine_negate_fusion
  10.6 0.1 sine_negate_fusion.1
  10.7 0.6 collective-permute-done
  11.3 0.8 copy-done.1
  12.1 5.6 %multiply_add_fusion.1 = f32[8,16,4096]{2,1,0:T(8,128)S(1)} fusion(bf16[8,16,4096]{2,1,0:T(8,128)(2,1)S(1)} %copy.37, bf16[8,7,4096]{2,1,0:T(8,128)(2,1)} %copy-done.1, f32[4096]{0:T(1024)S(1)} %bitcast.49, f32[4096]{0:T(1024)S(1)} %bitcast.50, f32[4096]{0:T(1024)S(1)} %bitcast.44, f32[4096]{0:T(1024)S(1)} %bitcast.45, f32[4096]{0:T(1024)S(1)} %bitcast.46, ...), kind=kLoop, calls=%fused_computation.16 | loop fusion | flops 23068672 | bytes 3735552 | tf_op jit(solution)/shard_map/add | solution.py:83
  17.7 3.0 reshape_reshape.3
  20.7 4.5 %copy.40 = f32[128,64,64]{0,1,2:T(8,128)S(1)} copy(f32[128,64,64]{2,1,0:T(8,128)} %reshape_reshape.3) | data formatting | bytes 4194304 | tf_op jit(solution)/shard_map/reshape;reshape | solution.py:34
  25.3 3.7 convolution_bitcast_fusion
  28.9 1.6 multiply_subtract_fusion
  30.5 0.6 pad_maximum_fusion
  31.1 4.9 %fusion.5 = bf16[128,64,64]{0,2,1:T(8,128)(2,1)S(1)} fusion(f32[128,64,128]{0,1,2:T(8,128)S(1)} %pad_maximum_fusion, f32[64,32]{0,1:T(8,128)S(1)} %get-tuple-element.22, f32[64,32]{0,1:T(8,128)S(1)} %get-tuple-element.21, f32[64,32]{0,1:T(8,128)S(1)} %fusion.46), kind=kOutput, calls=%fused_computation.23 | convolution fusion | flops 805855232 | bytes 5267456 | tf_op jit(solution)/shard_map/rkb,bm->rkm/dot_general | solution.py:52
  36.0 2.0 copy.44
  38.0 1.3 convert_element_type.81
  39.4 25.2 %all_to_all.5 = bf16[8,4,2,16,512]{4,3,2,0,1:T(8,128)(2,1)S(1)} all-to-all(bf16[8,4,2,16,512]{4,3,2,0,1:T(8,128)(2,1)S(1)} %copy.45), channel_id=1, replica_groups=mesh['chan'=4,'blk'=32] {'chan'}, dimensions={1} | all-to-all | bytes 2097152 | tf_op jit(solution)/shard_map/all_to_all | solution.py:90
  64.6 1.0 copy.63
  65.7 1.8 copy.50
  67.7 0.8 copy.51
  68.4 260.2 %all-gather.2.cloned.1.call-done = bf16[32,8,4,2,16,512]{5,4,3,2,1,0:T(8,128)(2,1)} async-done(((bf16[1,8,4,2,16,512]{5,4,3,2,1,0:T(8,128)(2,1)}), bf16[32,8,4,2,16,512]{5,4,3,2,1,0:T(8,128)(2,1)}) %all-gather.2.cloned.1.call-update) | async-done | bytes 33554448 | tf_op jit(solution)/shard_map/all_gather | solution.py:95
  328.6 41.9 %copy.54 = bf16[256,128,512,1]{1,0,3,2:T(8,128)(2,1)} copy(bf16[256,128,512,1]{2,1,0,3:T(8,128)(2,1)} %bitcast.35) | data formatting | bytes 67108864 | tf_op jit(solution)/shard_map/reshape | solution.py:68
  370.5 18.0 %multiply_bitcast_fusion = f32[2,8,256,512]{2,1,0,3:T(8,128)} fusion(bf16[256,128,512,1]{1,0,3,2:T(8,128)(2,1)} %copy.54, bf16[1,8,128,512]{2,1,0,3:T(8,128)(2,1)S(1)} %copy.51, bf16[1,8,128,512]{2,1,0,3:T(8,128)(2,1)S(1)} %copy.50), kind=kOutput, calls=%fused_computation | convolution fusion | flops 543162368 | bytes 44040192 | tf_op jit(solution)/shard_map/rikc,jkc->rijc/dot_general | solution.py:69
  388.5 9.9 %copy.53 = f32[2,8,256,512]{3,2,1,0:T(8,128)} copy(f32[2,8,256,512]{2,1,0,3:T(8,128)} %multiply_bitcast_fusion) | data formatting | bytes 16777216 | tf_op jit(solution)/shard_map/mul | solution.py:70
  (16 shorter events, 0.8 us)
Async XLA Ops:
  6.5 3.3 copy-start.2
  6.5 322.1 %all-gather.2.cloned.1.call-start = ((), (), s32[]{:S(2)}) async-start(), calls=%async_computation.1 | async-start | bytes 34603008 | tf_op jit(solution)/shard_map/all_gather | solution.py:95
  8.5 2.8 collective-permute-start
  11.3 0.8 copy-start.1
  65.6 1.8 copy-start
Sparse Core Ops, SparseCore 0:
  65.8 262.7 all-gather.1

commit v3 on v2

--- a/solution.py
+++ b/solution.py
@@ -58,15 +58,14 @@
 
 
 def correlate(own_block, every_block, inverse_count):
-    real_part, imag_part = own_block[:, :, 0], own_block[:, :, 1]
+    real_part, imag_part = own_block[:, :, :, 0], own_block[:, :, :, 1]
     paired = jnp.stack(
-        [jnp.stack([real_part, imag_part], axis=2), jnp.stack([imag_part, -real_part], axis=2)]
+        [jnp.stack([real_part, imag_part], axis=3), jnp.stack([imag_part, -real_part], axis=3)]
     )
-    blocks, feeds, spans, parts, frames, width = every_block.shape
-    depth = spans * parts * frames
-    left = paired.reshape(2, feeds, depth, width)
-    right = every_block.reshape(blocks * feeds, depth, width)
-    products = jnp.einsum("rikc,jkc->rijc", left, right, preferred_element_type=jnp.float32)
+    blocks, feeds, width, depth = every_block.shape
+    left = paired.reshape(2, feeds, width, depth)
+    right = every_block.reshape(blocks * feeds, width, depth)
+    products = jnp.einsum("rick,jck->rijc", left, right, preferred_element_type=jnp.float32)
     return products * inverse_count
 
 
@@ -89,8 +88,11 @@
     spectra = spectra.reshape(groups, feed_count, frame_count, 2, width).transpose(1, 0, 3, 2, 4)
     own_block = lax.all_to_all(spectra, "chan", split_axis=1, concat_axis=1, tiled=True)
     inverse_count = 1.0 / (groups * frame_count)
-    row_major = Layout(major_to_minor=tuple(range(own_block.ndim + 1)))
-    local = with_layout_constraint(own_block[None], row_major)
+    feeds, spans, parts, frames, width = own_block.shape
+    own_block = own_block.transpose(0, 4, 1, 2, 3)
+    local = own_block.reshape(1, feeds, width, spans * parts * frames)
+    row_major = Layout(major_to_minor=tuple(range(local.ndim)))
+    local = with_layout_constraint(local, row_major)
     every_block = with_layout_constraint(
         lax.all_gather(local, "blk", axis=0, tiled=True), row_major
     )

time: 407 us -> 371 us (0.912)
  local copies, waits for them, and re-layouts: 69.2 us -> 26.6 us
  matrix products: 26.6 us -> 33.3 us
    reshape x1 -> x2, local copies, waits for them, and re-layouts: 41.9 us -> 2.06 us  [on_device(): local = own_block.reshape(1, feeds, width, spans * parts * frames)]
    unnamed x0 -> x1, matrix products: none -> 24.7 us
    dot_general x1 -> x0, matrix products: 18 us -> none  [correlate(): jnp.einsum('rikc,jkc->rijc', left, right, preferred_element_type=jnp.floa...]
where the time goes in v3:
time: 371 us; the launch traced here: 370 us
  waiting for transfers between devices  262 us (71%)
  matrix products  33.3 us (9%)
  local copies, waits for them, and re-layouts  26.6 us (7%)
  blocking collectives  25.2 us (7%)
  between operations  13.6 us (4%)
  other arithmetic  8.58 us (2%)
    all_gather x1, waiting for transfers between devices, on_device(): lax.all_gather(local, 'blk', axis=0, tiled=True)  261 us
    all_to_all x1, blocking collectives, on_device(): lax.all_to_all(spectra, 'chan', split_axis=1, concat_axis=1, tiled=True)  25.2 us
    unnamed x1, matrix products  24.7 us
    mul x1, local copies, waits for them, and re-layouts, correlate(): return products * inverse_count  9.9 us
    another operation x2, local copies, waits for them, and re-layouts, spectra_of(): split = frames.reshape(rows, ROOT, ROOT)  7.53 us
  transfers between devices with their start and end apart: 2, of which 2 were waited for; matrix products, arithmetic and copies ran while one was open for 1% of the time, Pallas kernels for 0%

profile of v3, /device:TPU:0, one launch (start us, length us, event | category | flops | bytes accessed | tf_op | source)
XLA Modules:
  0.0 370.4 jit_solution(6149644430373038157)
XLA Ops:
  6.5 1.8 copy.24
  8.4 0.1 slice.81
  8.5 1.3 collective-permute-start
  10.0 0.1 fusion.45
  10.2 0.1 sine_negate_fusion
  10.6 0.1 sine_negate_fusion.1
  10.7 0.6 collective-permute-done
  11.3 0.8 copy-done
  12.1 5.6 %multiply_add_fusion.1 = f32[8,16,4096]{2,1,0:T(8,128)S(1)} fusion(bf16[8,16,4096]{2,1,0:T(8,128)(2,1)S(1)} %copy.24, bf16[8,7,4096]{2,1,0:T(8,128)(2,1)} %copy-done, f32[4096]{0:T(1024)S(1)} %bitcast.55, f32[4096]{0:T(1024)S(1)} %bitcast.56, f32[4096]{0:T(1024)S(1)} %bitcast.50, f32[4096]{0:T(1024)S(1)} %bitcast.51, f32[4096]{0:T(1024)S(1)} %bitcast.52, ...), kind=kLoop, calls=%fused_computation.19 | loop fusion | flops 23068672 | bytes 3735552 | tf_op jit(solution)/shard_map/add | solution.py:82
  17.8 3.0 reshape_reshape.3
  20.8 4.5 %copy.27 = f32[128,64,64]{0,1,2:T(8,128)S(1)} copy(f32[128,64,64]{2,1,0:T(8,128)} %reshape_reshape.3) | data formatting | bytes 4194304 | tf_op jit(solution)/shard_map/reshape;reshape | solution.py:34
  25.3 3.7 convolution_bitcast_fusion
  29.0 1.6 multiply_subtract_fusion
  30.6 0.6 pad_maximum_fusion
  31.2 4.9 %fusion.9 = bf16[128,64,64]{0,2,1:T(8,128)(2,1)S(1)} fusion(f32[128,64,128]{0,1,2:T(8,128)S(1)} %pad_maximum_fusion, f32[64,32]{0,1:T(8,128)S(1)} %get-tuple-element.20, f32[64,32]{0,1:T(8,128)S(1)} %get-tuple-element.19, f32[64,32]{0,1:T(8,128)S(1)} %fusion.50), kind=kOutput, calls=%fused_computation.26 | convolution fusion | flops 805855232 | bytes 5267456 | tf_op jit(solution)/shard_map/rkb,bm->rkm/dot_general | solution.py:52
  36.1 2.0 copy.31
  38.1 1.3 convert_element_type.81
  39.3 25.2 %all_to_all.5 = bf16[8,4,2,16,512]{4,3,0,2,1:T(8,128)(2,1)S(1)} all-to-all(bf16[8,4,2,16,512]{4,3,0,2,1:T(8,128)(2,1)S(1)} %bitcast.46), channel_id=1, replica_groups=mesh['chan'=4,'blk'=32] {'chan'}, dimensions={1} | all-to-all | bytes 2097152 | tf_op jit(solution)/shard_map/all_to_all | solution.py:89
  64.6 1.3 copy.33
  66.0 0.8 copy.35
  67.0 0.8 copy.36
  67.8 261.1 %all-gather.2.cloned.1.call-done = bf16[32,8,512,128]{3,2,1,0:T(8,128)(2,1)} async-done(((bf16[1,8,512,128]{3,2,1,0:T(8,128)(2,1)}), bf16[32,8,512,128]{3,2,1,0:T(8,128)(2,1)}) %all-gather.2.cloned.1.call-update) | async-done | bytes 33554448 | tf_op jit(solution)/shard_map/all_gather | solution.py:97
  328.9 24.7 %fusion.2 = f32[2,8,256,512]{2,1,0,3:T(8,128)} fusion(bf16[256,512,128]{2,1,0:T(8,128)(2,1)} %bitcast.57, bf16[1,8,512,128]{3,1,0,2:T(8,128)(2,1)S(1)} %copy.36, bf16[1,8,512,128]{3,1,0,2:T(8,128)(2,1)S(1)} %copy.35), kind=kOutput, calls=%fused_computation.3 | convolution fusion | flops 540016640 | bytes 44040192
  353.6 9.9 %copy.38 = f32[2,8,256,512]{3,2,1,0:T(8,128)} copy(f32[2,8,256,512]{2,1,0,3:T(8,128)} %fusion.2) | data formatting | bytes 16777216 | tf_op jit(solution)/shard_map/mul | solution.py:69
  (14 shorter events, 0.8 us)
Async XLA Ops:
  6.5 3.3 copy-start.1
  6.5 322.4 %all-gather.2.cloned.1.call-start = ((), (), s32[]{:S(2)}) async-start(), calls=%async_computation.1 | async-start | bytes 34603008 | tf_op jit(solution)/shard_map/all_gather | solution.py:97
  8.5 2.8 collective-permute-start
  11.3 0.8 copy-start
Sparse Core Ops, SparseCore 0:
  66.1 262.7 all-gather.1

commit v4 on v3

--- a/solution.py
+++ b/solution.py
@@ -92,11 +92,17 @@
     own_block = own_block.transpose(0, 4, 1, 2, 3)
     local = own_block.reshape(1, feeds, width, spans * parts * frames)
     row_major = Layout(major_to_minor=tuple(range(local.ndim)))
-    local = with_layout_constraint(local, row_major)
-    every_block = with_layout_constraint(
-        lax.all_gather(local, "blk", axis=0, tiled=True), row_major
-    )
-    return correlate(own_block, every_block, inverse_count)
+    pieces = []
+    piece_width = width // 2
+    for first in range(0, width, piece_width):
+        piece = with_layout_constraint(local[:, :, first : first + piece_width], row_major)
+        every_piece = with_layout_constraint(
+            lax.all_gather(piece, "blk", axis=0, tiled=True), row_major
+        )
+        pieces.append(
+            correlate(own_block[:, first : first + piece_width], every_piece, inverse_count)
+        )
+    return jnp.concatenate(pieces, axis=3)
 
 
 def solution(mesh):

time: 371 us -> 430 us (1.16); the launches traced: 370 us -> 423 us
  waiting for transfers between devices: 262 us -> 290 us
  matrix products: 33.3 us -> 51.7 us
    all_gather x1 -> x2, waiting for transfers between devices: 261 us -> 290 us  [on_device(): lax.all_gather(piece, 'blk', axis=0, tiled=True)]
    unnamed x1 -> x2, matrix products: 24.7 us -> 43.1 us
    concatenate x0 -> x1, local copies, waits for them, and re-layouts: none -> 9.9 us  [on_device(): return jnp.concatenate(pieces, axis=3)]
    mul x1 -> x0, local copies, waits for them, and re-layouts: 9.9 us -> none  [correlate(): return products * inverse_count]
  transfers between devices with their start and end apart: 2 -> 3, of which waited for: 2 -> 3; matrix products, arithmetic and copies ran while one was open for 1% -> 6% of each run, Pallas kernels for 0% -> 0%
where the time goes in v4:
time: 430 us; the launch traced here: 423 us
  waiting for transfers between devices  290 us (67%)
  matrix products  51.7 us (12%)
  local copies, waits for them, and re-layouts  27.5 us (6%)
  blocking collectives  25.2 us (6%)
  between operations  14.1 us (3%)
  other arithmetic  12.7 us (3%)
    all_gather x2, waiting for transfers between devices, on_device(): lax.all_gather(piece, 'blk', axis=0, tiled=True)  290 us
    unnamed x2, matrix products  43.1 us
    all_to_all x1, blocking collectives, on_device(): lax.all_to_all(spectra, 'chan', split_axis=1, concat_axis=1, tiled=True)  25.2 us
    concatenate x1, local copies, waits for them, and re-layouts, on_device(): return jnp.concatenate(pieces, axis=3)  9.9 us
  transfers between devices with their start and end apart: 3, of which 3 were waited for; matrix products, arithmetic and copies ran while one was open for 6% of the time, Pallas kernels for 0%

profile of v4, /device:TPU:0, one launch (start us, length us, event | category | flops | bytes accessed | tf_op | source)
XLA Modules:
  0.0 422.8 jit_solution(12620426090305650500)
XLA Ops:
  6.5 1.8 copy.35
  8.5 1.3 collective-permute-start
  10.7 0.6 collective-permute-done
  11.3 0.8 copy-done.1
  12.1 5.6 %multiply_add_fusion.1 = f32[8,16,4096]{2,1,0:T(8,128)S(1)} fusion(bf16[8,16,4096]{2,1,0:T(8,128)(2,1)S(1)} %copy.35, bf16[8,7,4096]{2,1,0:T(8,128)(2,1)} %copy-done.1, f32[4096]{0:T(1024)S(1)} %bitcast.73, f32[4096]{0:T(1024)S(1)} %bitcast.74, f32[4096]{0:T(1024)S(1)} %bitcast.68, f32[4096]{0:T(1024)S(1)} %bitcast.69, f32[4096]{0:T(1024)S(1)} %bitcast.70, ...), kind=kLoop, calls=%fused_computation.21 | loop fusion | flops 23068672 | bytes 3735552 | tf_op jit(solution)/shard_map/add | solution.py:82
  17.7 3.0 reshape_reshape.3
  20.7 4.5 %copy.38 = f32[128,64,64]{0,1,2:T(8,128)S(1)} copy(f32[128,64,64]{2,1,0:T(8,128)} %reshape_reshape.3) | data formatting | bytes 4194304 | tf_op jit(solution)/shard_map/reshape;reshape | solution.py:34
  25.3 3.7 convolution_bitcast_fusion
  28.9 1.6 multiply_subtract_fusion
  30.5 0.6 pad_maximum_fusion.1
  31.1 4.9 %fusion.12 = bf16[128,64,64]{0,2,1:T(8,128)(2,1)S(1)} fusion(f32[128,64,128]{0,1,2:T(8,128)S(1)} %pad_maximum_fusion.1, f32[64,32]{0,1:T(8,128)S(1)} %get-tuple-element.26, f32[64,32]{0,1:T(8,128)S(1)} %get-tuple-element.25, f32[64,32]{0,1:T(8,128)S(1)} %fusion.57), kind=kOutput, calls=%fused_computation.28 | convolution fusion | flops 805855232 | bytes 5267456 | tf_op jit(solution)/shard_map/rkb,bm->rkm/dot_general | solution.py:52
  36.0 2.0 copy.42
  38.0 1.3 convert_element_type.81
  39.3 25.2 %all_to_all.5 = bf16[8,4,2,16,512]{4,3,0,2,1:T(8,128)(2,1)S(1)} all-to-all(bf16[8,4,2,16,512]{4,3,0,2,1:T(8,128)(2,1)S(1)} %bitcast.60), channel_id=1, replica_groups=mesh['chan'=4,'blk'=32] {'chan'}, dimensions={1} | all-to-all | bytes 2097152 | tf_op jit(solution)/shard_map/all_to_all | solution.py:89
  64.7 1.0 copy.57
  65.8 1.0 copy.58
  67.9 0.3 copy.54
  68.3 0.3 copy.53
  68.7 155.1 %all-gather.3.cloned.1.call-done = bf16[32,8,256,128]{3,2,1,0:T(8,128)(2,1)} async-done(((bf16[1,8,256,128]{3,2,1,0:T(8,128)(2,1)}), bf16[32,8,256,128]{3,2,1,0:T(8,128)(2,1)}) %all-gather.3.cloned.1.call-update) | async-done | bytes 16777232 | tf_op jit(solution)/shard_map/all_gather | solution.py:100
  223.8 22.2 %fusion.5 = f32[2,8,256,256]{2,1,0,3:T(8,128)} fusion(bf16[256,256,128]{2,1,0:T(8,128)(2,1)} %bitcast.75, bf16[1,8,256,128]{3,1,0,2:T(8,128)(2,1)S(1)} %copy.48, bf16[1,8,256,128]{3,1,0,2:T(8,128)(2,1)S(1)} %copy.47), kind=kOutput, calls=%fused_computation.9 | convolution fusion | flops 270008320 | bytes 22020096
  245.9 134.6 %all-gather.5.cloned.1.call-done = bf16[32,8,256,128]{3,2,1,0:T(8,128)(2,1)} async-done(((bf16[1,8,256,128]{3,2,1,0:T(8,128)(2,1)}), bf16[32,8,256,128]{3,2,1,0:T(8,128)(2,1)}) %all-gather.5.cloned.1.call-update) | async-done | bytes 16777232 | tf_op jit(solution)/shard_map/all_gather | solution.py:100
  380.5 20.9 %fusion.4 = f32[2,8,256,256]{2,1,0,3:T(8,128)S(1)} fusion(bf16[256,256,128]{2,1,0:T(8,128)(2,1)} %bitcast.76, bf16[1,8,256,128]{3,1,0,2:T(8,128)(2,1)S(1)} %copy.54, bf16[1,8,256,128]{3,1,0,2:T(8,128)(2,1)S(1)} %copy.53), kind=kOutput, calls=%fused_computation.7 | convolution fusion | flops 270008320 | bytes 22020096
  401.4 4.2 pad_maximum_fusion
  405.6 9.9 %copy.56 = f32[2,8,256,512]{3,2,1,0:T(8,128)} copy(f32[2,8,256,512]{2,1,0,3:T(8,128)} %pad_maximum_fusion) | data formatting | bytes 16777216 | tf_op jit(solution)/shard_map/concatenate | solution.py:105
  (30 shorter events, 2.4 us)
Async XLA Ops:
  6.5 3.3 copy-start.2
  6.5 217.2 %all-gather.3.cloned.1.call-start = ((), (), s32[]{:S(2)}) async-start(), calls=%async_computation.1 | async-start | bytes 17301504 | tf_op jit(solution)/shard_map/all_gather | solution.py:100
  8.5 2.8 collective-permute-start
  11.3 0.8 copy-start.1
  65.7 314.8 %all-gather.5.cloned.1.call-start = ((), (), s32[]{:S(2)}) async-start(), calls=%async_computation.2 | async-start | bytes 17301504 | tf_op jit(solution)/shard_map/all_gather | solution.py:100
  380.5 20.9 %copy-start = (f32[2,8,256,256]{2,1,0,3:T(8,128)S(1)}, f32[2,8,256,256]{2,1,0,3:T(8,128)}, u32[]{:S(2)}) copy-start(f32[2,8,256,256]{2,1,0,3:T(8,128)} %fusion.5) | copy-start | bytes 12582916
Sparse Core Ops, SparseCore 0:
  65.8 157.8 all-gather.2
  226.7 153.7 all-gather.4

commit v5 on v3

--- a/solution.py
+++ b/solution.py
@@ -69,6 +69,20 @@
     return products * inverse_count
 
 
+def corner_turn(spectra, axis):
+    count = lax.axis_size(axis)
+    me = lax.axis_index(axis)
+    pieces = []
+    for steps in range(count):
+        outgoing = lax.dynamic_index_in_dim(spectra, (me + steps) % count, axis=1, keepdims=False)
+        if steps:
+            outgoing = lax.ppermute(
+                outgoing, axis, [(source, (source + steps) % count) for source in range(count)]
+            )
+        pieces.append(outgoing)
+    return jnp.stack(pieces, axis=1)
+
+
 def on_device(voltages, fir_taps):
     feed_count = voltages.shape[0]
     frame_count = voltages.shape[1] // L
@@ -86,7 +100,7 @@
     spectra = spectra_of(frame_rows, groups).astype(jnp.bfloat16)
     width = spectra.shape[-1]
     spectra = spectra.reshape(groups, feed_count, frame_count, 2, width).transpose(1, 0, 3, 2, 4)
-    own_block = lax.all_to_all(spectra, "chan", split_axis=1, concat_axis=1, tiled=True)
+    own_block = corner_turn(spectra, "chan")
     inverse_count = 1.0 / (groups * frame_count)
     feeds, spans, parts, frames, width = own_block.shape
     own_block = own_block.transpose(0, 4, 1, 2, 3)

time: 371 us -> 368 us (level)
  blocking collectives: 25.2 us -> 0 us
  waiting for transfers between devices: 262 us -> 274 us
  starting transfers between devices: 1.32 us -> 11.3 us
    all_to_all x1 -> x0, blocking collectives: 25.2 us -> none  [on_device(): lax.all_to_all(spectra, 'chan', split_axis=1, concat_axis=1, tiled=True)]
    ppermute x0 -> x3, waiting for transfers between devices: none -> 12.4 us  [corner_turn(): lax.ppermute(outgoing, axis, [(source, (source + steps) % count) for sour...]
    ppermute x0 -> x3, starting transfers between devices: none -> 10 us  [corner_turn(): lax.ppermute(outgoing, axis, [(source, (source + steps) % count) for sour...]
  transfers between devices with their start and end apart: 2 -> 5, of which waited for: 2 -> 3; matrix products, arithmetic and copies ran while one was open for 1% -> 1% of each run, Pallas kernels for 0% -> 0%
where the time goes in v5:
time: 368 us
  waiting for transfers between devices  274 us (74%)
  matrix products  33.3 us (9%)
  local copies, waits for them, and re-layouts  27 us (7%)
  between operations  13.6 us (4%)
  starting transfers between devices  11.3 us (3%)
  other arithmetic  8.71 us (2%)
    all_gather x1, waiting for transfers between devices, on_device(): lax.all_gather(local, 'blk', axis=0, tiled=True)  261 us
    unnamed x1, matrix products  24.7 us
    ppermute x3, waiting for transfers between devices, corner_turn(): lax.ppermute(outgoing, axis, [(source, (source + steps) % count) for sour...  12.4 us
    ppermute x3, starting transfers between devices, corner_turn(): lax.ppermute(outgoing, axis, [(source, (source + steps) % count) for sour...  10 us
    mul x1, local copies, waits for them, and re-layouts, correlate(): return products * inverse_count  9.9 us
    another operation x2, local copies, waits for them, and re-layouts, spectra_of(): split = frames.reshape(rows, ROOT, ROOT)  7.53 us
  transfers between devices with their start and end apart: 5, of which 3 were waited for; matrix products, arithmetic and copies ran while one was open for 1% of the time, Pallas kernels for 0%

profile of v5, /device:TPU:0, one launch (start us, length us, event | category | flops | bytes accessed | tf_op | source)
XLA Modules:
  0.0 368.0 jit_solution(8626789084454647909)
XLA Ops:
  6.5 1.8 copy.27
  8.5 1.3 collective-permute-start
  10.2 0.1 sine_negate_fusion
  10.6 0.1 sine_negate_fusion.1
  10.8 0.5 collective-permute-done
  11.3 0.8 copy-done
  12.1 5.6 %multiply_add_fusion.1 = f32[8,16,4096]{2,1,0:T(8,128)S(1)} fusion(bf16[8,16,4096]{2,1,0:T(8,128)(2,1)S(1)} %copy.27, bf16[8,7,4096]{2,1,0:T(8,128)(2,1)} %copy-done, f32[4096]{0:T(1024)S(1)} %bitcast.72, f32[4096]{0:T(1024)S(1)} %bitcast.73, f32[4096]{0:T(1024)S(1)} %bitcast.67, f32[4096]{0:T(1024)S(1)} %bitcast.68, f32[4096]{0:T(1024)S(1)} %bitcast.69, ...), kind=kLoop, calls=%fused_computation.19 | loop fusion | flops 23068672 | bytes 3735552 | tf_op jit(solution)/shard_map/add | solution.py:96
  17.8 3.0 reshape_reshape.3
  20.8 4.5 %copy.30 = f32[128,64,64]{0,1,2:T(8,128)S(1)} copy(f32[128,64,64]{2,1,0:T(8,128)} %reshape_reshape.3) | data formatting | bytes 4194304 | tf_op jit(solution)/shard_map/reshape;reshape | solution.py:34
  25.3 3.7 convolution_bitcast_fusion
  29.0 1.6 multiply_subtract_fusion
  30.6 0.6 pad_maximum_fusion
  31.2 4.9 %fusion.9 = bf16[128,64,64]{0,2,1:T(8,128)(2,1)S(1)} fusion(f32[128,64,128]{0,1,2:T(8,128)S(1)} %pad_maximum_fusion, f32[64,32]{0,1:T(8,128)S(1)} %get-tuple-element.24, f32[64,32]{0,1:T(8,128)S(1)} %get-tuple-element.23, f32[64,32]{0,1:T(8,128)S(1)} %fusion.50), kind=kOutput, calls=%fused_computation.26 | convolution fusion | flops 805855232 | bytes 5267456 | tf_op jit(solution)/shard_map/rkb,bm->rkm/dot_general | solution.py:52
  36.1 2.0 copy.34
  38.1 1.3 convert_element_type.81
  39.4 2.7 collective-permute-start.3
  42.1 7.2 %collective-permute-start.2 = (bf16[8,2,16,512]{3,2,0,1:T(8,128)(2,1)S(1)}, bf16[8,2,16,512]{3,2,0,1:T(8,128)(2,1)S(1)}, u32[]{:S(2)}, u32[]{:S(2)}) collective-permute-start(bf16[8,2,16,512]{3,2,0,1:T(8,128)(2,1)S(1)} %get-tuple-element.11), channel_id=1, source_target_pairs={{0,64},{32,96},{64,0},{96,32},{1,65},{33,97},{65,1},{97,33},{2,66}... | collective-permute-start | bytes 786440 | tf_op jit(solution)/shard_map/ppermute | solution.py:79
  49.5 12.4 %collective-permute-done.2 = bf16[8,2,16,512]{3,2,0,1:T(8,128)(2,1)S(1)} collective-permute-done((bf16[8,2,16,512]{3,2,0,1:T(8,128)(2,1)S(1)}, bf16[8,2,16,512]{3,2,0,1:T(8,128)(2,1)S(1)}, u32[]{:S(2)}, u32[]{:S(2)}) %collective-permute-start.2) | collective-permute-done | bytes 262176 | tf_op jit(solution)/shard_map/ppermute | solution.py:79
  62.0 1.5 copy.36
  63.6 0.8 copy.38
  64.6 0.8 copy.39
  65.4 261.1 %all-gather.2.cloned.1.call-done = bf16[32,8,512,128]{3,2,1,0:T(8,128)(2,1)} async-done(((bf16[1,8,512,128]{3,2,1,0:T(8,128)(2,1)}), bf16[32,8,512,128]{3,2,1,0:T(8,128)(2,1)}) %all-gather.2.cloned.1.call-update) | async-done | bytes 33554448 | tf_op jit(solution)/shard_map/all_gather | solution.py:111
  326.5 24.7 %fusion.2 = f32[2,8,256,512]{2,1,0,3:T(8,128)} fusion(bf16[256,512,128]{2,1,0:T(8,128)(2,1)} %bitcast.74, bf16[1,8,512,128]{3,1,0,2:T(8,128)(2,1)S(1)} %copy.39, bf16[1,8,512,128]{3,1,0,2:T(8,128)(2,1)S(1)} %copy.38), kind=kOutput, calls=%fused_computation.3 | convolution fusion | flops 540016640 | bytes 44040192
  351.3 9.9 %copy.41 = f32[2,8,256,512]{3,2,1,0:T(8,128)} copy(f32[2,8,256,512]{2,1,0,3:T(8,128)} %fusion.2) | data formatting | bytes 16777216 | tf_op jit(solution)/shard_map/mul | solution.py:69
  (21 shorter events, 1.4 us)
Async XLA Ops:
  6.5 3.3 copy-start.1
  6.5 320.0 %all-gather.2.cloned.1.call-start = ((), (), s32[]{:S(2)}) async-start(), calls=%async_computation | async-start | bytes 34603008 | tf_op jit(solution)/shard_map/all_gather | solution.py:111
  8.5 2.8 collective-permute-start
  11.3 0.8 copy-start
  39.4 10.0 %collective-permute-start.3 = (bf16[8,2,16,512]{3,2,0,1:T(8,128)(2,1)S(1)}, bf16[8,2,16,512]{3,2,0,1:T(8,128)(2,1)S(1)}, u32[]{:S(2)}, u32[]{:S(2)}) collective-permute-start(bf16[8,2,16,512]{3,2,0,1:T(8,128)(2,1)S(1)} %get-tuple-element.10), channel_id=1, source_target_pairs={{0,96},{32,0},{64,32},{96,64},{1,97},{33,1},{65,33},{97,65},{2,98}... | collective-permute-start | bytes 786440 | tf_op jit(solution)/shard_map/ppermute | solution.py:79
  42.1 19.7 %collective-permute-start.2 = (bf16[8,2,16,512]{3,2,0,1:T(8,128)(2,1)S(1)}, bf16[8,2,16,512]{3,2,0,1:T(8,128)(2,1)S(1)}, u32[]{:S(2)}, u32[]{:S(2)}) collective-permute-start(bf16[8,2,16,512]{3,2,0,1:T(8,128)(2,1)S(1)} %get-tuple-element.11), channel_id=1, source_target_pairs={{0,64},{32,96},{64,0},{96,32},{1,65},{33,97},{65,1},{97,33},{2,66}... | collective-permute-start | bytes 786440 | tf_op jit(solution)/shard_map/ppermute | solution.py:79
  49.3 12.5 %collective-permute-start.1 = (bf16[8,2,16,512]{3,2,0,1:T(8,128)(2,1)S(1)}, bf16[8,2,16,512]{3,2,0,1:T(8,128)(2,1)S(1)}, u32[]{:S(2)}, u32[]{:S(2)}) collective-permute-start(bf16[8,2,16,512]{3,2,0,1:T(8,128)(2,1)S(1)} %get-tuple-element.12), channel_id=1, source_target_pairs={{0,32},{32,64},{64,96},{96,0},{1,33},{33,65},{65,97},{97,1},{2,34}... | collective-permute-start | bytes 786440 | tf_op jit(solution)/shard_map/ppermute | solution.py:79
Sparse Core Ops, SparseCore 0:
  63.7 262.7 all-gather.1

commit v6 on v5

--- a/solution.py
+++ b/solution.py
@@ -10,6 +10,10 @@
 L = 4096
 C = 2048
 ROOT = 64
+CHAN = ("z_lo", "core")
+PLANE = "z_hi"
+WITHIN = ("y", "x")
+BLK = (PLANE,) + WITHIN
 
 
 def shifted(value, axis, steps):
@@ -86,10 +90,10 @@
 def on_device(voltages, fir_taps):
     feed_count = voltages.shape[0]
     frame_count = voltages.shape[1] // L
-    groups = lax.axis_size("chan")
+    groups = lax.axis_size(CHAN)
     own_frames = voltages.reshape(feed_count, frame_count, L)
     last_frames = own_frames[:, frame_count - (TAPS - 1) :, :]
-    earlier = shifted(last_frames, "chan", 1)
+    earlier = shifted(last_frames, CHAN, 1)
     extended = jnp.concatenate([earlier, own_frames], axis=1)
     filtered = jnp.zeros((feed_count, frame_count, L), jnp.float32)
     for tap_index in range(TAPS):
@@ -100,25 +104,40 @@
     spectra = spectra_of(frame_rows, groups).astype(jnp.bfloat16)
     width = spectra.shape[-1]
     spectra = spectra.reshape(groups, feed_count, frame_count, 2, width).transpose(1, 0, 3, 2, 4)
-    own_block = corner_turn(spectra, "chan")
+    own_block = corner_turn(spectra, CHAN)
     inverse_count = 1.0 / (groups * frame_count)
     feeds, spans, parts, frames, width = own_block.shape
     own_block = own_block.transpose(0, 4, 1, 2, 3)
     local = own_block.reshape(1, feeds, width, spans * parts * frames)
-    row_major = Layout(major_to_minor=tuple(range(local.ndim)))
-    local = with_layout_constraint(local, row_major)
-    every_block = with_layout_constraint(
-        lax.all_gather(local, "blk", axis=0, tiled=True), row_major
+    row_major = Layout(major_to_minor=tuple(range(local.ndim + 1)))
+    partner = lax.ppermute(local, PLANE, [(0, 1), (1, 0)])
+    first_plane = lax.axis_index(PLANE) == 0
+    pair = jnp.where(
+        first_plane,
+        jnp.concatenate([local, partner], axis=0),
+        jnp.concatenate([partner, local], axis=0),
     )
-    return correlate(own_block, every_block, inverse_count)
+    pair = with_layout_constraint(pair[None], row_major)
+    gathered = with_layout_constraint(
+        lax.all_gather(pair, WITHIN, axis=0, tiled=True), row_major
+    )
+    every_block = gathered.reshape((-1,) + local.shape[1:])
+    products = correlate(own_block, every_block, inverse_count)
+    parts, feeds, _, width = products.shape
+    products = products.reshape(parts, feeds, gathered.shape[0], 2, feeds, width)
+    return products.transpose(0, 1, 3, 2, 4, 5).reshape(parts, feeds, -1, width)
 
 
 def solution(mesh):
-    placed = (P("blk", "chan"), P())
+    chan_axes, blk_axes = mesh.devices.shape
+    split = jax.sharding.Mesh(
+        mesh.devices.reshape(2, chan_axes // 2, 2, 4, blk_axes // 8), CHAN + BLK
+    )
+    placed = (P(BLK, CHAN), P())
     return jax.shard_map(
         on_device,
-        mesh=mesh,
+        mesh=split,
         in_specs=placed,
-        out_specs=P(None, "blk", None, "chan"),
+        out_specs=P(None, BLK, None, CHAN),
         check_vma=False,
     )

time: 368 us -> 341 us (0.927)
  waiting for transfers between devices: 274 us -> 231 us
  local copies, waits for them, and re-layouts: 27 us -> 35.7 us
    all_gather x1, waiting for transfers between devices: 261 us -> 198 us  [on_device(): lax.all_gather(pair, WITHIN, axis=0, tiled=True)]
    ppermute x0 -> x1, waiting for transfers between devices: none -> 19.5 us  [on_device(): partner = lax.ppermute(local, PLANE, [(0, 1), (1, 0)])]
    transpose x0 -> x1, local copies, waits for them, and re-layouts: none -> 8.21 us  [on_device(): return products.transpose(0, 1, 3, 2, 4, 5).reshape(parts, feeds, -1, width)]
  transfers between devices with their start and end apart: 5 -> 6, of which waited for: 3 -> 4; matrix products, arithmetic and copies ran while one was open for 1% -> 1% of each run, Pallas kernels for 0% -> 0%
where the time goes in v6:
time: 341 us; the launch traced here: 340 us
  waiting for transfers between devices  231 us (68%)
  local copies, waits for them, and re-layouts  35.7 us (10%)
  matrix products  33.4 us (10%)
  starting transfers between devices  14.9 us (4%)
  between operations  13.6 us (4%)
  other arithmetic  11.8 us (3%)
    all_gather x1, waiting for transfers between devices, on_device(): lax.all_gather(pair, WITHIN, axis=0, tiled=True)  198 us
    unnamed x1, matrix products  24.7 us
    ppermute x1, waiting for transfers between devices, on_device(): partner = lax.ppermute(local, PLANE, [(0, 1), (1, 0)])  19.5 us
    ppermute x3, waiting for transfers between devices, corner_turn(): lax.ppermute(outgoing, axis, [(source, (source + steps) % count) for sour...  12.4 us
    ppermute x3, starting transfers between devices, corner_turn(): lax.ppermute(outgoing, axis, [(source, (source + steps) % count) for sour...  10 us
    mul x1, local copies, waits for them, and re-layouts, correlate(): return products * inverse_count  9.99 us
    transpose x1, local copies, waits for them, and re-layouts, on_device(): return products.transpose(0, 1, 3, 2, 4, 5).reshape(parts, feeds, -1, width)  8.21 us
    another operation x2, local copies, waits for them, and re-layouts, spectra_of(): split = frames.reshape(rows, ROOT, ROOT)  7.53 us
  transfers between devices with their start and end apart: 6, of which 4 were waited for; matrix products, arithmetic and copies ran while one was open for 1% of the time, Pallas kernels for 0%

profile of v6, /device:TPU:0, one launch (start us, length us, event | category | flops | bytes accessed | tf_op | source)
XLA Modules:
  0.0 340.1 jit_solution(11549093101219308029)
XLA Ops:
  6.5 1.8 copy.49
  8.5 1.3 collective-permute-start
  11.3 0.8 copy-done
  12.1 5.6 %multiply_add_fusion.1 = f32[8,16,4096]{2,1,0:T(8,128)S(1)} fusion(bf16[8,16,4096]{2,1,0:T(8,128)(2,1)S(1)} %copy.49, bf16[8,7,4096]{2,1,0:T(8,128)(2,1)} %copy-done, f32[4096]{0:T(1024)S(1)} %bitcast.80, f32[4096]{0:T(1024)S(1)} %bitcast.81, f32[4096]{0:T(1024)S(1)} %bitcast.75, f32[4096]{0:T(1024)S(1)} %bitcast.76, f32[4096]{0:T(1024)S(1)} %bitcast.77, ...), kind=kLoop, calls=%fused_computation.20 | loop fusion | flops 23068672 | bytes 3735552 | tf_op jit(solution)/shard_map/add | solution.py:100
  17.7 3.0 reshape_reshape.6
  20.7 4.5 %copy.52 = f32[128,64,64]{0,1,2:T(8,128)S(1)} copy(f32[128,64,64]{2,1,0:T(8,128)} %reshape_reshape.6) | data formatting | bytes 4194304 | tf_op jit(solution)/shard_map/reshape;reshape | solution.py:38
  25.3 3.7 %convolution_bitcast_fusion = f32[128,128,64]{0,1,2:T(8,128)S(1)} fusion(f32[128,64,64]{0,1,2:T(8,128)S(1)} %copy.52, f32[64,64]{1,0:T(8,128)S(1)} %get-tuple-element.21, f32[64,64]{1,0:T(8,128)S(1)} %get-tuple-element.22), kind=kOutput, calls=%fused_computation.13 | convolution fusion | flops 805322752 | bytes 6324224 | tf_op jit(solution)/shard_map/rab,ak->rkb/dot_general | solution.py:39
  28.9 1.6 multiply_subtract_fusion
  31.1 4.9 %fusion.9 = bf16[128,64,64]{0,2,1:T(8,128)(2,1)S(1)} fusion(f32[128,64,128]{0,1,2:T(8,128)S(1)} %pad_maximum_fusion, f32[64,32]{0,1:T(8,128)S(1)} %get-tuple-element.24, f32[64,32]{0,1:T(8,128)S(1)} %get-tuple-element.23, f32[64,32]{0,1:T(8,128)S(1)} %fusion.50), kind=kOutput, calls=%fused_computation.27 | convolution fusion | flops 805855232 | bytes 5267456 | tf_op jit(solution)/shard_map/rkb,bm->rkm/dot_general | solution.py:56
  36.1 2.0 copy.56
  38.0 1.3 convert_element_type.81
  39.4 2.7 collective-permute-start.3
  42.1 7.2 %collective-permute-start.2 = (bf16[8,2,16,512]{3,2,0,1:T(8,128)(2,1)S(1)}, bf16[8,2,16,512]{3,2,0,1:T(8,128)(2,1)S(1)}, u32[]{:S(2)}, u32[]{:S(2)}) collective-permute-start(bf16[8,2,16,512]{3,2,0,1:T(8,128)(2,1)S(1)} %get-tuple-element.11), channel_id=1, source_target_pairs={{0,64},{32,96},{64,0},{96,32},{1,65},{33,97},{65,1},{97,33},{2,66}... | collective-permute-start | bytes 786440 | tf_op jit(solution)/shard_map/ppermute | solution.py:83
  49.4 12.4 %collective-permute-done.2 = bf16[8,2,16,512]{3,2,0,1:T(8,128)(2,1)S(1)} collective-permute-done((bf16[8,2,16,512]{3,2,0,1:T(8,128)(2,1)S(1)}, bf16[8,2,16,512]{3,2,0,1:T(8,128)(2,1)S(1)}, u32[]{:S(2)}, u32[]{:S(2)}) %collective-permute-start.2) | collective-permute-done | bytes 262176 | tf_op jit(solution)/shard_map/ppermute | solution.py:83
  62.0 1.3 copy.59
  63.3 3.6 %collective-permute-start.4 = (bf16[1,8,512,128]{3,2,1,0:T(8,128)(2,1)}, bf16[1,8,512,128]{3,2,1,0:T(8,128)(2,1)}, u32[]{:S(2)}, u32[]{:S(2)}) collective-permute-start(bf16[1,8,512,128]{3,2,1,0:T(8,128)(2,1)} %copy.59), channel_id=1, source_target_pairs={{0,16},{16,0},{1,17},{17,1},{2,18},{18,2},{3,19},{19,3},{4,20},{20... | collective-permute-start | bytes 3145736 | tf_op jit(solution)/shard_map/ppermute | solution.py:113
  67.6 19.5 %collective-permute-done.4 = bf16[1,8,512,128]{3,2,1,0:T(8,128)(2,1)} collective-permute-done((bf16[1,8,512,128]{3,2,1,0:T(8,128)(2,1)}, bf16[1,8,512,128]{3,2,1,0:T(8,128)(2,1)}, u32[]{:S(2)}, u32[]{:S(2)}) %collective-permute-start.4) | collective-permute-done | bytes 1048608 | tf_op jit(solution)/shard_map/ppermute | solution.py:113
  87.1 3.2 maximum_select_fusion
  90.3 0.8 copy.63
  91.3 0.8 copy.64
  92.1 198.2 %all-gather.2.cloned.1.call-done = bf16[16,2,8,512,128]{4,3,2,1,0:T(8,128)(2,1)} async-done(((bf16[1,2,8,512,128]{4,3,2,1,0:T(8,128)(2,1)}), bf16[16,2,8,512,128]{4,3,2,1,0:T(8,128)(2,1)}) %all-gather.2.cloned.1.call-update) | async-done | bytes 33554448 | tf_op jit(solution)/shard_map/all_gather | solution.py:122
  290.3 24.7 %fusion.2 = f32[2,8,256,512]{2,1,0,3:T(8,128)} fusion(bf16[256,512,128]{2,1,0:T(8,128)(2,1)} %bitcast.82, bf16[1,8,512,128]{3,1,0,2:T(8,128)(2,1)S(1)} %copy.64, bf16[1,8,512,128]{3,1,0,2:T(8,128)(2,1)S(1)} %copy.63), kind=kOutput, calls=%fused_computation.3 | convolution fusion | flops 540016640 | bytes 44040192
  315.1 10.0 %copy.66 = f32[2,8,256,512]{3,2,1,0:T(8,128)} copy(f32[2,8,256,512]{2,1,0,3:T(8,128)} %fusion.2) | data formatting | bytes 16777216 | tf_op jit(solution)/shard_map/mul | solution.py:73
  325.1 8.2 %copy.67 = f32[2,8,2,16,8,512]{5,4,3,2,1,0:T(8,128)} copy(f32[2,8,2,16,8,512]{5,4,2,3,1,0:T(8,128)} %bitcast.63) | data formatting | bytes 16777216 | tf_op jit(solution)/shard_map/transpose | solution.py:128
  (26 shorter events, 3.5 us)
Async XLA Ops:
  6.5 3.3 copy-start.1
  6.5 283.8 %all-gather.2.cloned.1.call-start = ((), (), s32[]{:S(2)}) async-start(), calls=%async_computation | async-start | bytes 35651584 | tf_op jit(solution)/shard_map/all_gather | solution.py:122
  8.5 2.8 collective-permute-start
  11.3 0.8 copy-start
  39.4 10.0 %collective-permute-start.3 = (bf16[8,2,16,512]{3,2,0,1:T(8,128)(2,1)S(1)}, bf16[8,2,16,512]{3,2,0,1:T(8,128)(2,1)S(1)}, u32[]{:S(2)}, u32[]{:S(2)}) collective-permute-start(bf16[8,2,16,512]{3,2,0,1:T(8,128)(2,1)S(1)} %get-tuple-element.10), channel_id=1, source_target_pairs={{0,96},{32,0},{64,32},{96,64},{1,97},{33,1},{65,33},{97,65},{2,98}... | collective-permute-start | bytes 786440 | tf_op jit(solution)/shard_map/ppermute | solution.py:83
  42.1 19.7 %collective-permute-start.2 = (bf16[8,2,16,512]{3,2,0,1:T(8,128)(2,1)S(1)}, bf16[8,2,16,512]{3,2,0,1:T(8,128)(2,1)S(1)}, u32[]{:S(2)}, u32[]{:S(2)}) collective-permute-start(bf16[8,2,16,512]{3,2,0,1:T(8,128)(2,1)S(1)} %get-tuple-element.11), channel_id=1, source_target_pairs={{0,64},{32,96},{64,0},{96,32},{1,65},{33,97},{65,1},{97,33},{2,66}... | collective-permute-start | bytes 786440 | tf_op jit(solution)/shard_map/ppermute | solution.py:83
  49.3 12.5 %collective-permute-start.1 = (bf16[8,2,16,512]{3,2,0,1:T(8,128)(2,1)S(1)}, bf16[8,2,16,512]{3,2,0,1:T(8,128)(2,1)S(1)}, u32[]{:S(2)}, u32[]{:S(2)}) collective-permute-start(bf16[8,2,16,512]{3,2,0,1:T(8,128)(2,1)S(1)} %get-tuple-element.12), channel_id=1, source_target_pairs={{0,32},{32,64},{64,96},{96,0},{1,33},{33,65},{65,97},{97,1},{2,34}... | collective-permute-start | bytes 786440 | tf_op jit(solution)/shard_map/ppermute | solution.py:83
  63.3 23.8 %collective-permute-start.4 = (bf16[1,8,512,128]{3,2,1,0:T(8,128)(2,1)}, bf16[1,8,512,128]{3,2,1,0:T(8,128)(2,1)}, u32[]{:S(2)}, u32[]{:S(2)}) collective-permute-start(bf16[1,8,512,128]{3,2,1,0:T(8,128)(2,1)} %copy.59), channel_id=1, source_target_pairs={{0,16},{16,0},{1,17},{17,1},{2,18},{18,2},{3,19},{19,3},{4,20},{20... | collective-permute-start | bytes 3145736 | tf_op jit(solution)/shard_map/ppermute | solution.py:113
Sparse Core Ops, SparseCore 0:
  90.4 199.8 all-gather.1

commit v7 on v6

--- a/solution.py
+++ b/solution.py
@@ -66,25 +66,31 @@
     paired = jnp.stack(
         [jnp.stack([real_part, imag_part], axis=3), jnp.stack([imag_part, -real_part], axis=3)]
     )
-    blocks, feeds, width, depth = every_block.shape
-    left = paired.reshape(2, feeds, width, depth)
-    right = every_block.reshape(blocks * feeds, width, depth)
-    products = jnp.einsum("rick,jck->rijc", left, right, preferred_element_type=jnp.float32)
+    left = paired.reshape((2,) + own_block.shape[:2] + (-1,))
+    products = jnp.einsum("rick,jck->rijc", left, every_block, preferred_element_type=jnp.float32)
     return products * inverse_count
 
 
-def corner_turn(spectra, axis):
-    count = lax.axis_size(axis)
-    me = lax.axis_index(axis)
-    pieces = []
-    for steps in range(count):
-        outgoing = lax.dynamic_index_in_dim(spectra, (me + steps) % count, axis=1, keepdims=False)
-        if steps:
-            outgoing = lax.ppermute(
-                outgoing, axis, [(source, (source + steps) % count) for source in range(count)]
+def corner_turn(spectra):
+    count = lax.axis_size(CHAN)
+    me = lax.axis_index(CHAN)
+    planes = []
+    for flip in range(2):
+        pieces = []
+        for steps in range(count):
+            outgoing = lax.dynamic_index_in_dim(
+                spectra, (me + steps) % count, axis=1, keepdims=False
             )
-        pieces.append(outgoing)
-    return jnp.stack(pieces, axis=1)
+            if steps or flip:
+                pairs = [
+                    (source * 2 + plane, ((source + steps) % count) * 2 + (plane ^ flip))
+                    for source in range(count)
+                    for plane in range(2)
+                ]
+                outgoing = lax.ppermute(outgoing, CHAN + (PLANE,), pairs)
+            pieces.append(outgoing)
+        planes.append(jnp.stack(pieces, axis=1))
+    return planes
 
 
 def on_device(voltages, fir_taps):
@@ -104,28 +110,27 @@
     spectra = spectra_of(frame_rows, groups).astype(jnp.bfloat16)
     width = spectra.shape[-1]
     spectra = spectra.reshape(groups, feed_count, frame_count, 2, width).transpose(1, 0, 3, 2, 4)
-    own_block = corner_turn(spectra, CHAN)
+    own_block, partner_block = corner_turn(spectra)
     inverse_count = 1.0 / (groups * frame_count)
     feeds, spans, parts, frames, width = own_block.shape
+
     own_block = own_block.transpose(0, 4, 1, 2, 3)
-    local = own_block.reshape(1, feeds, width, spans * parts * frames)
-    row_major = Layout(major_to_minor=tuple(range(local.ndim + 1)))
-    partner = lax.ppermute(local, PLANE, [(0, 1), (1, 0)])
+    partner_block = partner_block.transpose(0, 4, 1, 2, 3)
+    row_major = Layout(major_to_minor=tuple(range(5)))
     first_plane = lax.axis_index(PLANE) == 0
     pair = jnp.where(
         first_plane,
-        jnp.concatenate([local, partner], axis=0),
-        jnp.concatenate([partner, local], axis=0),
+        jnp.stack([own_block, partner_block]),
+        jnp.stack([partner_block, own_block]),
     )
-    pair = with_layout_constraint(pair[None], row_major)
+    pair = with_layout_constraint(
+        pair.reshape(2, 1, feeds, width, spans * parts * frames), row_major
+    )
     gathered = with_layout_constraint(
-        lax.all_gather(pair, WITHIN, axis=0, tiled=True), row_major
+        lax.all_gather(pair, WITHIN, axis=1, tiled=True), row_major
     )
-    every_block = gathered.reshape((-1,) + local.shape[1:])
-    products = correlate(own_block, every_block, inverse_count)
-    parts, feeds, _, width = products.shape
-    products = products.reshape(parts, feeds, gathered.shape[0], 2, feeds, width)
-    return products.transpose(0, 1, 3, 2, 4, 5).reshape(parts, feeds, -1, width)
+    every_block = gathered.reshape((-1,) + gathered.shape[3:])
+    return correlate(own_block, every_block, inverse_count)
 
 
 def solution(mesh):

time: 341 us -> 319 us (0.935)
  waiting for transfers between devices: 231 us -> 203 us
  starting transfers between devices: 14.9 us -> 26.9 us
  local copies, waits for them, and re-layouts: 35.7 us -> 27.8 us
    ppermute x4 -> x7, waiting for transfers between devices: 31.9 us -> 7.34 us  [corner_turn(): outgoing = lax.ppermute(outgoing, CHAN + (PLANE,), pairs)]
    ppermute x4 -> x7, starting transfers between devices: 13.6 us -> 25.6 us  [corner_turn(): outgoing = lax.ppermute(outgoing, CHAN + (PLANE,), pairs)]
    transpose x1, local copies, waits for them, and re-layouts: 8.21 us -> 0.09 us  [on_device(): partner_block = partner_block.transpose(0, 4, 1, 2, 3)]
  transfers between devices with their start and end apart: 6 -> 9, of which waited for: 4 -> 5; matrix products, arithmetic and copies ran while one was open for 1% -> 1% of each run, Pallas kernels for 0% -> 0%
where the time goes in v7:
time: 319 us; the launch traced here: 318 us
  waiting for transfers between devices  203 us (64%)
  matrix products  33.4 us (10%)
  local copies, waits for them, and re-layouts  27.8 us (9%)
  starting transfers between devices  26.9 us (8%)
  between operations  13.7 us (4%)
  other arithmetic  13.1 us (4%)
    all_gather x1, waiting for transfers between devices, on_device(): lax.all_gather(pair, WITHIN, axis=1, tiled=True)  195 us
    ppermute x7, starting transfers between devices, corner_turn(): outgoing = lax.ppermute(outgoing, CHAN + (PLANE,), pairs)  25.6 us
    unnamed x1, matrix products  24.8 us
    mul x1, local copies, waits for them, and re-layouts, correlate(): return products * inverse_count  9.9 us
    another operation x2, local copies, waits for them, and re-layouts, spectra_of(): split = frames.reshape(rows, ROOT, ROOT)  7.53 us
    ppermute x7, waiting for transfers between devices, corner_turn(): outgoing = lax.ppermute(outgoing, CHAN + (PLANE,), pairs)  7.34 us
  transfers between devices with their start and end apart: 9, of which 5 were waited for; matrix products, arithmetic and copies ran while one was open for 1% of the time, Pallas kernels for 0%

profile of v7, /device:TPU:0, one launch (start us, length us, event | category | flops | bytes accessed | tf_op | source)
XLA Modules:
  0.0 318.1 jit_solution(18325690180993722560)
XLA Ops:
  6.5 1.8 copy.14
  8.5 1.3 collective-permute-start
  12.1 5.6 %multiply_add_fusion.1 = f32[8,16,4096]{2,1,0:T(8,128)S(1)} fusion(bf16[8,16,4096]{2,1,0:T(8,128)(2,1)S(1)} %copy.14, bf16[8,7,4096]{2,1,0:T(8,128)(2,1)} %copy-done, f32[4096]{0:T(1024)S(1)} %bitcast.86, f32[4096]{0:T(1024)S(1)} %bitcast.87, f32[4096]{0:T(1024)S(1)} %bitcast.81, f32[4096]{0:T(1024)S(1)} %bitcast.82, f32[4096]{0:T(1024)S(1)} %bitcast.83, ...), kind=kLoop, calls=%fused_computation.20 | loop fusion | flops 23068672 | bytes 3735552 | tf_op jit(solution)/shard_map/add | solution.py:106
  17.8 3.0 reshape_reshape.3
  20.8 4.5 %copy.17 = f32[128,64,64]{0,1,2:T(8,128)S(1)} copy(f32[128,64,64]{2,1,0:T(8,128)} %reshape_reshape.3) | data formatting | bytes 4194304 | tf_op jit(solution)/shard_map/reshape;reshape | solution.py:38
  25.3 3.7 %convolution_bitcast_fusion = f32[128,128,64]{0,1,2:T(8,128)S(1)} fusion(f32[128,64,64]{0,1,2:T(8,128)S(1)} %copy.17, f32[64,64]{1,0:T(8,128)S(1)} %get-tuple-element.22, f32[64,64]{1,0:T(8,128)S(1)} %get-tuple-element.23), kind=kOutput, calls=%fused_computation.13 | convolution fusion | flops 805322752 | bytes 6324224 | tf_op jit(solution)/shard_map/rab,ak->rkb/dot_general | solution.py:39
  29.0 1.6 multiply_subtract_fusion
  31.2 4.9 %fusion.9 = bf16[128,64,64]{0,2,1:T(8,128)(2,1)S(1)} fusion(f32[128,64,128]{0,1,2:T(8,128)S(1)} %pad_maximum_fusion, f32[64,32]{0,1:T(8,128)S(1)} %get-tuple-element.25, f32[64,32]{0,1:T(8,128)S(1)} %get-tuple-element.24, f32[64,32]{0,1:T(8,128)S(1)} %fusion.50), kind=kOutput, calls=%fused_computation.27 | convolution fusion | flops 805855232 | bytes 5267456 | tf_op jit(solution)/shard_map/rkb,bm->rkm/dot_general | solution.py:56
  36.1 2.0 copy.21
  38.1 1.3 convert_element_type.81
  39.5 4.5 %collective-permute-start.4 = (bf16[8,2,16,512]{3,2,0,1:T(8,128)(2,1)S(1)}, bf16[8,2,16,512]{3,2,0,1:T(8,128)(2,1)S(1)}, u32[]{:S(2)}, u32[]{:S(2)}) collective-permute-start(bf16[8,2,16,512]{3,2,0,1:T(8,128)(2,1)S(1)} %get-tuple-element.10), channel_id=1, source_target_pairs={{0,16},{16,0},{32,48},{48,32},{64,80},{80,64},{96,112},{112,96},{1... | collective-permute-start | bytes 786440 | tf_op jit(solution)/shard_map/ppermute | solution.py:90
  44.6 8.5 %collective-permute-start.6 = (bf16[8,2,16,512]{3,2,0,1:T(8,128)(2,1)S(1)}, bf16[8,2,16,512]{3,2,0,1:T(8,128)(2,1)S(1)}, u32[]{:S(2)}, u32[]{:S(2)}) collective-permute-start(bf16[8,2,16,512]{3,2,0,1:T(8,128)(2,1)S(1)} %get-tuple-element.12), channel_id=1, source_target_pairs={{0,80},{16,64},{32,112},{48,96},{64,16},{80,0},{96,48},{112,32},{1... | collective-permute-start | bytes 786440 | tf_op jit(solution)/shard_map/ppermute | solution.py:90
  53.1 1.3 collective-permute-start.5
  54.3 4.7 %collective-permute-start.2 = (bf16[8,2,16,512]{3,2,0,1:T(8,128)(2,1)S(1)}, bf16[8,2,16,512]{3,2,0,1:T(8,128)(2,1)}, u32[]{:S(2)}, u32[]{:S(2)}) collective-permute-start(bf16[8,2,16,512]{3,2,0,1:T(8,128)(2,1)S(1)} %get-tuple-element.12), channel_id=1, source_target_pairs={{0,64},{16,80},{32,96},{48,112},{64,0},{80,16},{96,32},{112,48},{1... | collective-permute-start | bytes 786440 | tf_op jit(solution)/shard_map/ppermute | solution.py:90
  59.0 6.1 %collective-permute-start.1 = (bf16[8,2,16,512]{3,2,0,1:T(8,128)(2,1)S(1)}, bf16[8,2,16,512]{3,2,0,1:T(8,128)(2,1)}, u32[]{:S(2)}, u32[]{:S(2)}) collective-permute-start(bf16[8,2,16,512]{3,2,0,1:T(8,128)(2,1)S(1)} %get-tuple-element.13), channel_id=1, source_target_pairs={{0,32},{16,48},{32,64},{48,80},{64,96},{80,112},{96,0},{112,16},{1... | collective-permute-start | bytes 786440 | tf_op jit(solution)/shard_map/ppermute | solution.py:90
  65.1 5.8 %collective-permute-done.6 = bf16[8,2,16,512]{3,2,0,1:T(8,128)(2,1)S(1)} collective-permute-done((bf16[8,2,16,512]{3,2,0,1:T(8,128)(2,1)S(1)}, bf16[8,2,16,512]{3,2,0,1:T(8,128)(2,1)S(1)}, u32[]{:S(2)}, u32[]{:S(2)}) %collective-permute-start.6) | collective-permute-done | bytes 262176 | tf_op jit(solution)/shard_map/ppermute | solution.py:90
  71.2 0.9 copy.25
  72.1 1.4 collective-permute-done.2
  73.6 1.2 maximum_bitcast_fusion.2
  74.8 1.3 copy.24
  76.2 3.3 %maximum_select_fusion = bf16[2,1,8,512,128]{4,3,2,1,0:T(8,128)(2,1)} fusion(bf16[1,1,8,512,128]{4,3,2,1,0:T(8,128)(2,1)S(1)} %copy.25, bf16[1,1,8,512,128]{4,3,2,1,0:T(8,128)(2,1)} %copy.24, pred[]{:T(512)S(6)} %eq.17), kind=kLoop, calls=%fused_computation.14 | loop fusion | flops 3145728 | bytes 4194305 | tf_op jit(solution)/shard_map/jit(_where)/select_n | solution.py:121
  81.3 195.4 %all-gather.2.cloned.1.call-done = bf16[2,16,8,512,128]{4,3,2,1,0:T(8,128)(2,1)} async-done(((bf16[2,1,8,512,128]{4,3,2,1,0:T(8,128)(2,1)}), bf16[2,16,8,512,128]{4,3,2,1,0:T(8,128)(2,1)}) %all-gather.2.cloned.1.call-update) | async-done | bytes 33554448 | tf_op jit(solution)/shard_map/all_gather | solution.py:130
  276.6 24.8 %fusion.2 = f32[2,8,256,512]{2,1,0,3:T(8,128)} fusion(bf16[256,512,128]{2,1,0:T(8,128)(2,1)} %bitcast.88, bf16[1,8,512,128]{3,1,0,2:T(8,128)(2,1)S(1)} %copy.31, bf16[1,8,512,128]{3,1,0,2:T(8,128)(2,1)S(1)} %copy.30), kind=kOutput, calls=%fused_computation.3 | convolution fusion | flops 540016640 | bytes 44040192
  301.4 9.9 %copy.33 = f32[2,8,256,512]{3,2,1,0:T(8,128)} copy(f32[2,8,256,512]{2,1,0,3:T(8,128)} %fusion.2) | data formatting | bytes 16777216 | tf_op jit(solution)/shard_map/mul | solution.py:71
  (33 shorter events, 5.8 us)
Async XLA Ops:
  6.5 3.3 %copy-start.1 = (f32[8,4096]{1,0:T(8,128)S(1)}, f32[8,4096]{1,0:T(8,128)}, u32[]{:S(2)}) copy-start(f32[8,4096]{1,0:T(8,128)} %param.3) | copy-start | bytes 393220
  6.5 270.1 %all-gather.2.cloned.1.call-start = ((), (), s32[]{:S(2)}) async-start(), calls=%async_computation | async-start | bytes 35651584 | tf_op jit(solution)/shard_map/all_gather | solution.py:130
  8.5 2.8 collective-permute-start
  11.3 0.8 copy-start
  39.5 14.8 %collective-permute-start.4 = (bf16[8,2,16,512]{3,2,0,1:T(8,128)(2,1)S(1)}, bf16[8,2,16,512]{3,2,0,1:T(8,128)(2,1)S(1)}, u32[]{:S(2)}, u32[]{:S(2)}) collective-permute-start(bf16[8,2,16,512]{3,2,0,1:T(8,128)(2,1)S(1)} %get-tuple-element.10), channel_id=1, source_target_pairs={{0,16},{16,0},{32,48},{48,32},{64,80},{80,64},{96,112},{112,96},{1... | collective-permute-start | bytes 786440 | tf_op jit(solution)/shard_map/ppermute | solution.py:90
  44.0 15.0 %collective-permute-start.7 = (bf16[8,2,16,512]{3,2,0,1:T(8,128)(2,1)S(1)}, bf16[8,2,16,512]{3,2,0,1:T(8,128)(2,1)S(1)}, u32[]{:S(2)}, u32[]{:S(2)}) collective-permute-start(bf16[8,2,16,512]{3,2,0,1:T(8,128)(2,1)S(1)} %get-tuple-element.11), channel_id=1, source_target_pairs={{0,112},{16,96},{32,16},{48,0},{64,48},{80,32},{96,80},{112,64},{1... | collective-permute-start | bytes 786440 | tf_op jit(solution)/shard_map/ppermute | solution.py:90
  44.6 26.3 %collective-permute-start.6 = (bf16[8,2,16,512]{3,2,0,1:T(8,128)(2,1)S(1)}, bf16[8,2,16,512]{3,2,0,1:T(8,128)(2,1)S(1)}, u32[]{:S(2)}, u32[]{:S(2)}) collective-permute-start(bf16[8,2,16,512]{3,2,0,1:T(8,128)(2,1)S(1)} %get-tuple-element.12), channel_id=1, source_target_pairs={{0,80},{16,64},{32,112},{48,96},{64,16},{80,0},{96,48},{112,32},{1... | collective-permute-start | bytes 786440 | tf_op jit(solution)/shard_map/ppermute | solution.py:90
  53.1 18.0 %collective-permute-start.5 = (bf16[8,2,16,512]{3,2,0,1:T(8,128)(2,1)S(1)}, bf16[8,2,16,512]{3,2,0,1:T(8,128)(2,1)S(1)}, u32[]{:S(2)}, u32[]{:S(2)}) collective-permute-start(bf16[8,2,16,512]{3,2,0,1:T(8,128)(2,1)S(1)} %get-tuple-element.13), channel_id=1, source_target_pairs={{0,48},{16,32},{32,80},{48,64},{64,112},{80,96},{96,16},{112,0},{1... | collective-permute-start | bytes 786440 | tf_op jit(solution)/shard_map/ppermute | solution.py:90
  54.3 17.8 %collective-permute-start.3 = (bf16[8,2,16,512]{3,2,0,1:T(8,128)(2,1)S(1)}, bf16[8,2,16,512]{3,2,0,1:T(8,128)(2,1)S(1)}, u32[]{:S(2)}, u32[]{:S(2)}) collective-permute-start(bf16[8,2,16,512]{3,2,0,1:T(8,128)(2,1)S(1)} %get-tuple-element.11), channel_id=1, source_target_pairs={{0,96},{16,112},{32,0},{48,16},{64,32},{80,48},{96,64},{112,80},{1... | collective-permute-start | bytes 786440 | tf_op jit(solution)/shard_map/ppermute | solution.py:90
  54.3 19.3 %collective-permute-start.2 = (bf16[8,2,16,512]{3,2,0,1:T(8,128)(2,1)S(1)}, bf16[8,2,16,512]{3,2,0,1:T(8,128)(2,1)}, u32[]{:S(2)}, u32[]{:S(2)}) collective-permute-start(bf16[8,2,16,512]{3,2,0,1:T(8,128)(2,1)S(1)} %get-tuple-element.12), channel_id=1, source_target_pairs={{0,64},{16,80},{32,96},{48,112},{64,0},{80,16},{96,32},{112,48},{1... | collective-permute-start | bytes 786440 | tf_op jit(solution)/shard_map/ppermute | solution.py:90
  59.0 14.6 %collective-permute-start.1 = (bf16[8,2,16,512]{3,2,0,1:T(8,128)(2,1)S(1)}, bf16[8,2,16,512]{3,2,0,1:T(8,128)(2,1)}, u32[]{:S(2)}, u32[]{:S(2)}) collective-permute-start(bf16[8,2,16,512]{3,2,0,1:T(8,128)(2,1)S(1)} %get-tuple-element.13), channel_id=1, source_target_pairs={{0,32},{16,48},{32,64},{48,80},{64,96},{80,112},{96,0},{112,16},{1... | collective-permute-start | bytes 786440 | tf_op jit(solution)/shard_map/ppermute | solution.py:90
Sparse Core Ops, SparseCore 0:
  79.6 196.9 all-gather.1

commit v8 on v7

--- a/solution.py
+++ b/solution.py
@@ -116,21 +116,23 @@
 
     own_block = own_block.transpose(0, 4, 1, 2, 3)
     partner_block = partner_block.transpose(0, 4, 1, 2, 3)
-    row_major = Layout(major_to_minor=tuple(range(5)))
-    first_plane = lax.axis_index(PLANE) == 0
-    pair = jnp.where(
-        first_plane,
-        jnp.stack([own_block, partner_block]),
-        jnp.stack([partner_block, own_block]),
-    )
-    pair = with_layout_constraint(
-        pair.reshape(2, 1, feeds, width, spans * parts * frames), row_major
+    row_major = Layout(major_to_minor=tuple(range(4)))
+    local = with_layout_constraint(
+        own_block.reshape(1, feeds, width, spans * parts * frames), row_major
     )
     gathered = with_layout_constraint(
-        lax.all_gather(pair, WITHIN, axis=1, tiled=True), row_major
+        lax.all_gather(local, WITHIN, axis=0, tiled=True), row_major
     )
-    every_block = gathered.reshape((-1,) + gathered.shape[3:])
-    return correlate(own_block, every_block, inverse_count)
+    plane_blocks = gathered.reshape((-1,) + gathered.shape[2:])
+    partner_part = correlate(partner_block, plane_blocks, inverse_count)
+    other_part = lax.ppermute(partner_part, PLANE, [(0, 1), (1, 0)])
+    own_part = correlate(own_block, plane_blocks, inverse_count)
+    first_plane = lax.axis_index(PLANE) == 0
+    return jnp.where(
+        first_plane,
+        jnp.concatenate([own_part, other_part], axis=2),
+        jnp.concatenate([other_part, own_part], axis=2),
+    )
 
 
 def solution(mesh):

time: 319 us -> 317 us (level)
  waiting for transfers between devices: 203 us -> 190 us
  matrix products: 33.4 us -> 43.1 us
  starting transfers between devices: 26.9 us -> 21.3 us
  local copies, waits for them, and re-layouts: 27.8 us -> 32.6 us
    all_gather x1, waiting for transfers between devices: 195 us -> 83.3 us  [on_device(): lax.all_gather(local, WITHIN, axis=0, tiled=True)]
    ppermute x0 -> x1, waiting for transfers between devices: none -> 76 us  [on_device(): other_part = lax.ppermute(partner_part, PLANE, [(0, 1), (1, 0)])]
    ppermute x7, waiting for transfers between devices: 7.34 us -> 29.9 us  [corner_turn(): outgoing = lax.ppermute(outgoing, CHAN + (PLANE,), pairs)]
    select_n x0 -> x1, local copies, waits for them, and re-layouts: none -> 9.9 us  [on_device(): jnp.where(first_plane, jnp.concatenate([own_part, other_part], axis=2), j...]
    mul x1 -> x0, local copies, waits for them, and re-layouts: 9.9 us -> none  [correlate(): return products * inverse_count]
    unnamed x1 -> x2, matrix products: 24.8 us -> 34.5 us
    ppermute x7, starting transfers between devices: 25.6 us -> 16.8 us  [corner_turn(): outgoing = lax.ppermute(outgoing, CHAN + (PLANE,), pairs)]
    select_n x1, other arithmetic: 3.26 us -> 7.1 us  [on_device(): jnp.where(first_plane, jnp.concatenate([own_part, other_part], axis=2), j...]
  transfers between devices with their start and end apart: 9 -> 10, of which waited for: 5 -> 7; matrix products, arithmetic and copies ran while one was open for 1% -> 7% of each run, Pallas kernels for 0% -> 0%
where the time goes in v8:
time: 317 us
  waiting for transfers between devices  190 us (60%)
  matrix products  43.1 us (14%)
  local copies, waits for them, and re-layouts  32.6 us (10%)
  starting transfers between devices  21.3 us (7%)
  other arithmetic  16.1 us (5%)
  between operations  13.7 us (4%)
    all_gather x1, waiting for transfers between devices, on_device(): lax.all_gather(local, WITHIN, axis=0, tiled=True)  83.3 us
    ppermute x1, waiting for transfers between devices, on_device(): other_part = lax.ppermute(partner_part, PLANE, [(0, 1), (1, 0)])  76 us
    unnamed x2, matrix products  34.5 us
    ppermute x7, waiting for transfers between devices, corner_turn(): outgoing = lax.ppermute(outgoing, CHAN + (PLANE,), pairs)  29.9 us
    ppermute x7, starting transfers between devices, corner_turn(): outgoing = lax.ppermute(outgoing, CHAN + (PLANE,), pairs)  16.8 us
    select_n x1, local copies, waits for them, and re-layouts, on_device(): jnp.where(first_plane, jnp.concatenate([own_part, other_part], axis=2), j...  9.9 us
    another operation x2, local copies, waits for them, and re-layouts, spectra_of(): split = frames.reshape(rows, ROOT, ROOT)  7.53 us
    select_n x1, other arithmetic, on_device(): jnp.where(first_plane, jnp.concatenate([own_part, other_part], axis=2), j...  7.1 us
  transfers between devices with their start and end apart: 10, of which 7 were waited for; matrix products, arithmetic and copies ran while one was open for 7% of the time, Pallas kernels for 0%

profile of v8, /device:TPU:0, one launch (start us, length us, event | category | flops | bytes accessed | tf_op | source)
XLA Modules:
  0.0 316.5 jit_solution(15600083964424306252)
XLA Ops:
  6.5 1.8 copy.35
  12.1 5.6 %multiply_add_fusion.1 = f32[8,16,4096]{2,1,0:T(8,128)S(1)} fusion(bf16[8,16,4096]{2,1,0:T(8,128)(2,1)S(1)} %copy.35, bf16[8,7,4096]{2,1,0:T(8,128)(2,1)} %copy-done, f32[4096]{0:T(1024)S(1)} %bitcast.100, f32[4096]{0:T(1024)S(1)} %bitcast.101, f32[4096]{0:T(1024)S(1)} %bitcast.95, f32[4096]{0:T(1024)S(1)} %bitcast.96, f32[4096]{0:T(1024)S(1)} %bitcast.97, ...), kind=kLoop, calls=%fused_computation.27 | loop fusion | flops 23068672 | bytes 3735552 | tf_op jit(solution)/shard_map/add | solution.py:106
  17.7 3.0 reshape_reshape.3
  20.8 4.5 %copy.38 = f32[128,64,64]{0,1,2:T(8,128)S(1)} copy(f32[128,64,64]{2,1,0:T(8,128)} %reshape_reshape.3) | data formatting | bytes 4194304 | tf_op jit(solution)/shard_map/reshape;reshape | solution.py:38
  25.3 3.7 %convolution_bitcast_fusion = f32[128,128,64]{0,1,2:T(8,128)S(1)} fusion(f32[128,64,64]{0,1,2:T(8,128)S(1)} %copy.38, f32[64,64]{1,0:T(8,128)S(1)} %get-tuple-element.24, f32[64,64]{1,0:T(8,128)S(1)} %get-tuple-element.25), kind=kOutput, calls=%fused_computation.18 | convolution fusion | flops 805322752 | bytes 6324224 | tf_op jit(solution)/shard_map/rab,ak->rkb/dot_general | solution.py:39
  28.9 1.6 multiply_subtract_fusion
  31.1 4.9 %fusion.16 = bf16[128,64,64]{0,2,1:T(8,128)(2,1)S(1)} fusion(f32[128,64,128]{0,1,2:T(8,128)S(1)} %pad_maximum_fusion, f32[64,32]{0,1:T(8,128)S(1)} %get-tuple-element.27, f32[64,32]{0,1:T(8,128)S(1)} %get-tuple-element.26, f32[64,32]{0,1:T(8,128)S(1)} %fusion.57), kind=kOutput, calls=%fused_computation.34 | convolution fusion | flops 805855232 | bytes 5267456 | tf_op jit(solution)/shard_map/rkb,bm->rkm/dot_general | solution.py:56
  36.1 2.0 copy.42
  40.2 2.6 collective-permute-start.3
  42.8 7.1 %collective-permute-start.2 = (bf16[8,2,16,512]{3,2,0,1:T(8,128)(2,1)S(1)}, bf16[8,2,16,512]{3,2,0,1:T(8,128)(2,1)S(1)}, u32[]{:S(2)}, u32[]{:S(2)}) collective-permute-start(bf16[8,2,16,512]{3,2,0,1:T(8,128)(2,1)S(1)} %get-tuple-element.13), channel_id=1, source_target_pairs={{0,64},{16,80},{32,96},{48,112},{64,0},{80,16},{96,32},{112,48},{1... | collective-permute-start | bytes 786440 | tf_op jit(solution)/shard_map/ppermute | solution.py:90
  50.1 12.4 %collective-permute-done.2 = bf16[8,2,16,512]{3,2,0,1:T(8,128)(2,1)S(1)} collective-permute-done((bf16[8,2,16,512]{3,2,0,1:T(8,128)(2,1)S(1)}, bf16[8,2,16,512]{3,2,0,1:T(8,128)(2,1)S(1)}, u32[]{:S(2)}, u32[]{:S(2)}) %collective-permute-start.2) | collective-permute-done | bytes 262176 | tf_op jit(solution)/shard_map/ppermute | solution.py:90
  64.1 3.7 %collective-permute-start.4 = (bf16[8,2,16,512]{3,2,0,1:T(8,128)(2,1)S(1)}, bf16[8,2,16,512]{3,2,0,1:T(8,128)(2,1)S(1)}, u32[]{:S(2)}, u32[]{:S(2)}) collective-permute-start(bf16[8,2,16,512]{3,2,0,1:T(8,128)(2,1)S(1)} %copy-done.5), channel_id=1, source_target_pairs={{0,16},{16,0},{32,48},{48,32},{64,80},{80,64},{96,112},{112,96},{1... | collective-permute-start | bytes 786440 | tf_op jit(solution)/shard_map/ppermute | solution.py:90
  67.9 3.2 collective-permute-start.5
  71.0 3.0 collective-permute-done.4
  74.0 8.9 %collective-permute-done.7 = bf16[8,2,16,512]{3,2,0,1:T(8,128)(2,1)S(1)} collective-permute-done((bf16[8,2,16,512]{3,2,0,1:T(8,128)(2,1)S(1)}, bf16[8,2,16,512]{3,2,0,1:T(8,128)(2,1)S(1)}, u32[]{:S(2)}, u32[]{:S(2)}) %collective-permute-start.7) | collective-permute-done | bytes 262176 | tf_op jit(solution)/shard_map/ppermute | solution.py:90
  82.9 5.6 %collective-permute-done.6 = bf16[8,2,16,512]{3,2,0,1:T(8,128)(2,1)S(1)} collective-permute-done((bf16[8,2,16,512]{3,2,0,1:T(8,128)(2,1)S(1)}, bf16[8,2,16,512]{3,2,0,1:T(8,128)(2,1)S(1)}, u32[]{:S(2)}, u32[]{:S(2)}) %collective-permute-start.6) | collective-permute-done | bytes 262176 | tf_op jit(solution)/shard_map/ppermute | solution.py:90
  89.8 2.4 copy.51
  94.0 83.3 %all-gather.2.cloned.1.call-done = bf16[16,8,512,128]{3,2,1,0:T(8,128)(2,1)} async-done(((bf16[1,8,512,128]{3,2,1,0:T(8,128)(2,1)}), bf16[16,8,512,128]{3,2,1,0:T(8,128)(2,1)}) %all-gather.2.cloned.1.call-update) | async-done | bytes 16777232 | tf_op jit(solution)/shard_map/all_gather | solution.py:124
  177.2 21.5 %fusion.4 = f32[2,8,128,512]{2,1,0,3:T(8,128)} fusion(bf16[128,512,128]{2,1,0:T(8,128)(2,1)} %bitcast.102, bf16[1,8,512,128]{3,1,0,2:T(8,128)(2,1)} %copy.52, bf16[1,8,512,128]{3,1,0,2:T(8,128)(2,1)} %copy.51), kind=kOutput, calls=%fused_computation.7 | convolution fusion | flops 270532608 | bytes 23068672
  198.7 3.1 collective-permute-start.8
  203.6 13.0 %fusion.5 = f32[2,8,128,512]{2,1,0,3:T(8,128)S(1)} fusion(bf16[128,512,128]{2,1,0:T(8,128)(2,1)} %bitcast.103, bf16[1,8,512,128]{3,1,0,2:T(8,128)(2,1)S(1)} %copy.47, bf16[1,8,512,128]{3,1,0,2:T(8,128)(2,1)S(1)} %copy.46), kind=kOutput, calls=%fused_computation.9 | convolution fusion | flops 270532608 | bytes 23068672
  216.6 76.0 %collective-permute-done.8 = f32[2,8,128,512]{2,1,0,3:T(8,128)} collective-permute-done((f32[2,8,128,512]{2,1,0,3:T(8,128)}, f32[2,8,128,512]{2,1,0,3:T(8,128)}, u32[]{:S(2)}, u32[]{:S(2)}) %collective-permute-start.8) | collective-permute-done | bytes 4194336 | tf_op jit(solution)/shard_map/ppermute | solution.py:128
  292.7 7.1 %maximum_select_fusion = f32[2,8,256,512]{2,1,0,3:T(8,128)} fusion(f32[2,8,128,512]{2,1,0,3:T(8,128)} %collective-permute-done.8, f32[2,8,128,512]{2,1,0,3:T(8,128)S(1)} %fusion.5, pred[]{:T(512)S(6)} %eq.17), kind=kLoop, calls=%fused_computation.4 | loop fusion | flops 6291456 | bytes 16777216 | tf_op jit(solution)/shard_map/jit(_where)/select_n | solution.py:131
  299.8 9.9 %copy.54 = f32[2,8,256,512]{3,2,1,0:T(8,128)} copy(f32[2,8,256,512]{2,1,0,3:T(8,128)} %maximum_select_fusion) | data formatting | bytes 16777216 | tf_op jit(solution)/shard_map/jit(_where)/select_n | solution.py:131
  (50 shorter events, 12.9 us)
Async XLA Ops:
  6.5 3.3 %copy-start.6 = (f32[8,4096]{1,0:T(8,128)S(1)}, f32[8,4096]{1,0:T(8,128)}, u32[]{:S(2)}) copy-start(f32[8,4096]{1,0:T(8,128)} %param.3) | copy-start | bytes 393220
  6.5 170.7 %all-gather.2.cloned.1.call-start = ((), (), s32[]{:S(2)}) async-start(), calls=%async_computation | async-start | bytes 17825792 | tf_op jit(solution)/shard_map/all_gather | solution.py:124
  8.5 2.8 collective-permute-start
  11.3 0.8 copy-start
  40.2 22.3 %copy-start.1 = (bf16[8,2,16,512]{3,2,0,1:T(8,128)(2,1)}, bf16[8,2,16,512]{3,2,0,1:T(8,128)(2,1)S(1)}, u32[]{:S(2)}) copy-start(bf16[8,2,16,512]{3,2,0,1:T(8,128)(2,1)S(1)} %get-tuple-element.13) | copy-start | bytes 786436
  40.2 22.3 %copy-start.3 = (bf16[8,2,16,512]{3,2,0,1:T(8,128)(2,1)}, bf16[8,2,16,512]{3,2,0,1:T(8,128)(2,1)S(1)}, u32[]{:S(2)}) copy-start(bf16[8,2,16,512]{3,2,0,1:T(8,128)(2,1)S(1)} %get-tuple-element.12) | copy-start | bytes 786436
  40.2 9.9 %collective-permute-start.3 = (bf16[8,2,16,512]{3,2,0,1:T(8,128)(2,1)S(1)}, bf16[8,2,16,512]{3,2,0,1:T(8,128)(2,1)S(1)}, u32[]{:S(2)}, u32[]{:S(2)}) collective-permute-start(bf16[8,2,16,512]{3,2,0,1:T(8,128)(2,1)S(1)} %get-tuple-element.12), channel_id=1, source_target_pairs={{0,96},{16,112},{32,0},{48,16},{64,32},{80,48},{96,64},{112,80},{1... | collective-permute-start | bytes 786440 | tf_op jit(solution)/shard_map/ppermute | solution.py:90
  42.8 19.7 %collective-permute-start.2 = (bf16[8,2,16,512]{3,2,0,1:T(8,128)(2,1)S(1)}, bf16[8,2,16,512]{3,2,0,1:T(8,128)(2,1)S(1)}, u32[]{:S(2)}, u32[]{:S(2)}) collective-permute-start(bf16[8,2,16,512]{3,2,0,1:T(8,128)(2,1)S(1)} %get-tuple-element.13), channel_id=1, source_target_pairs={{0,64},{16,80},{32,96},{48,112},{64,0},{80,16},{96,32},{112,48},{1... | collective-permute-start | bytes 786440 | tf_op jit(solution)/shard_map/ppermute | solution.py:90
  49.9 12.6 %collective-permute-start.1 = (bf16[8,2,16,512]{3,2,0,1:T(8,128)(2,1)S(1)}, bf16[8,2,16,512]{3,2,0,1:T(8,128)(2,1)S(1)}, u32[]{:S(2)}, u32[]{:S(2)}) collective-permute-start(bf16[8,2,16,512]{3,2,0,1:T(8,128)(2,1)S(1)} %get-tuple-element.14), channel_id=1, source_target_pairs={{0,32},{16,48},{32,64},{48,80},{64,96},{80,112},{96,0},{112,16},{1... | collective-permute-start | bytes 786440 | tf_op jit(solution)/shard_map/ppermute | solution.py:90
  62.7 1.4 copy-start.5
  62.7 5.0 %copy-start.4 = (bf16[8,2,16,512]{3,2,0,1:T(8,128)(2,1)S(1)}, bf16[8,2,16,512]{3,2,0,1:T(8,128)(2,1)}, u32[]{:S(2)}) copy-start(bf16[8,2,16,512]{3,2,0,1:T(8,128)(2,1)} %copy-done.3) | copy-start | bytes 786436
  62.7 5.0 %copy-start.2 = (bf16[8,2,16,512]{3,2,0,1:T(8,128)(2,1)S(1)}, bf16[8,2,16,512]{3,2,0,1:T(8,128)(2,1)}, u32[]{:S(2)}) copy-start(bf16[8,2,16,512]{3,2,0,1:T(8,128)(2,1)} %copy-done.1) | copy-start | bytes 786436
  64.1 9.9 %collective-permute-start.4 = (bf16[8,2,16,512]{3,2,0,1:T(8,128)(2,1)S(1)}, bf16[8,2,16,512]{3,2,0,1:T(8,128)(2,1)S(1)}, u32[]{:S(2)}, u32[]{:S(2)}) collective-permute-start(bf16[8,2,16,512]{3,2,0,1:T(8,128)(2,1)S(1)} %copy-done.5), channel_id=1, source_target_pairs={{0,16},{16,0},{32,48},{48,32},{64,80},{80,64},{96,112},{112,96},{1... | collective-permute-start | bytes 786440 | tf_op jit(solution)/shard_map/ppermute | solution.py:90
  67.8 15.2 %collective-permute-start.7 = (bf16[8,2,16,512]{3,2,0,1:T(8,128)(2,1)S(1)}, bf16[8,2,16,512]{3,2,0,1:T(8,128)(2,1)S(1)}, u32[]{:S(2)}, u32[]{:S(2)}) collective-permute-start(bf16[8,2,16,512]{3,2,0,1:T(8,128)(2,1)S(1)} %copy-done.4), channel_id=1, source_target_pairs={{0,112},{16,96},{32,16},{48,0},{64,48},{80,32},{96,80},{112,64},{1... | collective-permute-start | bytes 786440 | tf_op jit(solution)/shard_map/ppermute | solution.py:90
  67.8 20.8 %collective-permute-start.6 = (bf16[8,2,16,512]{3,2,0,1:T(8,128)(2,1)S(1)}, bf16[8,2,16,512]{3,2,0,1:T(8,128)(2,1)S(1)}, u32[]{:S(2)}, u32[]{:S(2)}) collective-permute-start(bf16[8,2,16,512]{3,2,0,1:T(8,128)(2,1)S(1)} %copy-done.2), channel_id=1, source_target_pairs={{0,80},{16,64},{32,112},{48,96},{64,16},{80,0},{96,48},{112,32},{1... | collective-permute-start | bytes 786440 | tf_op jit(solution)/shard_map/ppermute | solution.py:90
  67.9 20.7 %collective-permute-start.5 = (bf16[8,2,16,512]{3,2,0,1:T(8,128)(2,1)S(1)}, bf16[8,2,16,512]{3,2,0,1:T(8,128)(2,1)S(1)}, u32[]{:S(2)}, u32[]{:S(2)}) collective-permute-start(bf16[8,2,16,512]{3,2,0,1:T(8,128)(2,1)S(1)} %get-tuple-element.14), channel_id=1, source_target_pairs={{0,48},{16,32},{32,80},{48,64},{64,112},{80,96},{96,16},{112,0},{1... | collective-permute-start | bytes 786440 | tf_op jit(solution)/shard_map/ppermute | solution.py:90
  198.7 94.0 %collective-permute-start.8 = (f32[2,8,128,512]{2,1,0,3:T(8,128)}, f32[2,8,128,512]{2,1,0,3:T(8,128)}, u32[]{:S(2)}, u32[]{:S(2)}) collective-permute-start(f32[2,8,128,512]{2,1,0,3:T(8,128)} %fusion.4), channel_id=1, source_target_pairs={{0,16},{16,0},{1,17},{17,1},{2,18},{18,2},{3,19},{19,3},{4,20},{20... | collective-permute-start | bytes 12582920 | tf_op jit(solution)/shard_map/ppermute | solution.py:128
Sparse Core Ops, SparseCore 0:
  64.2 112.9 all-gather.1
